TPU v7x, 256 devices: a whole 4x4x8 slice. The times are simulated.
256 devices in a mesh: ctx: 64 (over y_lo, z, x), fsdp: 4 (over y_hi, core).
Axes of the slice: x: 4, y: 4 (y_hi: 2, y_lo: 2; y = y_hi * 2 + y_lo), z: 8, core: 2. Of those that a mesh axis runs over, the one named last changes fastest.
Arguments:
- query: bfloat16 [16384, 2048], P('ctx', 'fsdp'), may hold values from -11 to 11
- key: bfloat16 [16384, 2048], P('ctx', 'fsdp'), may hold values from -11 to 11
- value: bfloat16 [16384, 2048], P('ctx', 'fsdp'), may hold values from -6 to 6
- doc_ids: int32 [16384], P('ctx'), may hold values from 0 to 19, never falling along the last dimension, each value on 1 to 2048 neighbouring positions
- out_weight: bfloat16 [2048, 4096], P(('fsdp', 'ctx')), may hold values from -0.125 to 0.125
- grad_out: bfloat16 [16384, 4096], P('ctx', 'fsdp'), may hold values from -6 to 6
Outputs:
- grad_query: bfloat16 [16384, 2048], P('ctx', 'fsdp')
- grad_key: bfloat16 [16384, 2048], P('ctx', 'fsdp')
- grad_value: bfloat16 [16384, 2048], P('ctx', 'fsdp')
- grad_out_weight: float32 [2048, 4096], P(('fsdp', 'ctx'))
Inputs may be any that keep to these rules, and one draw needn't show every extreme that they name: `doc_ids`: document ids never fall along the sequence; every document has 1 to 2048 tokens and one has exactly 2048.
All inputs are finite; a program needn't handle non-finite values.
Results may differ from a plain program's by a relative error of at most 0.034.
Values may be sent and summed in bfloat16 or wider, within the bound.
No kernel may reach another device: no remote copies, remote signals or barrier semaphores. Data moves between devices by JAX's collectives and lax.ppermute only.
A program may use at most 128 MiB of HBM per device.

v0:
```python
import math

import jax
import jax.numpy as jnp
from jax import lax
from jax.sharding import PartitionSpec as P

DH = 128


NEGATIVE = -1e30


def shifted(array, axis, by):
    devices = lax.axis_size(axis)
    pairs = [(i, i + by) for i in range(devices) if 0 <= i + by < devices]
    return lax.ppermute(array, axis, pairs)


def as_sent(array):

    def short(part):
        return part.astype(jnp.bfloat16) if part.dtype == jnp.float32 else part

    return jax.tree.map(short, array)


def passed_along(block, axis, distance):
    devices = range(lax.axis_size(axis))
    route = [((i - distance) % len(devices), i) for i in devices]
    return lax.ppermute(block, axis, route)


def shards(query, key, value, doc_ids, out_weight, grad_out):
    tok_rows = query.shape[0]
    feature_width = query.shape[1]
    head_count = feature_width // DH
    cycle_size = lax.axis_size("ctx")
    cycle_reach = max(cycle_size // 8, 2)
    cycle_index = lax.axis_index("ctx")
    score_scale = 1.0 / math.sqrt(DH)
    local_pos = jnp.arange(tok_rows, dtype=jnp.int32)
    own_pos = cycle_index * tok_rows + local_pos
    own_docs = doc_ids + 1
    query_heads = query.reshape(tok_rows, head_count, DH)
    key_heads = key.reshape(tok_rows, head_count, DH)
    value_heads = value.reshape(tok_rows, head_count, DH)

    def scores_of(query_block, key_block):
        return (
            jnp.einsum("tnd,snd->nts", query_block, key_block, preferred_element_type=jnp.float32)
            * score_scale
        )

    state = (
        jnp.full((head_count, tok_rows), NEGATIVE, jnp.float32),
        jnp.zeros((head_count, tok_rows), jnp.float32),
        jnp.zeros((head_count, tok_rows, DH), jnp.float32),
    )
    key_block, value_block = (key_heads, value_heads)
    key_docs = own_docs
    stored_blocks = []
    for cycle_step in range(cycle_reach + 1):
        if cycle_step > 0:
            key_block, value_block = shifted((key_block, value_block), "ctx", 1)
            key_docs = shifted(key_docs, "ctx", 1)
        key_pos = own_pos - cycle_step * tok_rows
        pair_mask = (own_docs[:, None] == key_docs[None, :]) & (
            key_pos[None, :] <= own_pos[:, None]
        )
        forward_row_max, forward_row_sum, forward_output_sum = state
        forward_scores = jnp.where(pair_mask[None], scores_of(query_heads, key_block), NEGATIVE)
        new_max = jnp.maximum(forward_row_max, jnp.max(forward_scores, axis=-1))
        decay_factor = jnp.exp(forward_row_max - new_max)
        forward_weights = jnp.where(
            pair_mask[None], jnp.exp(forward_scores - new_max[..., None]), 0.0
        )
        new_sum = forward_row_sum * decay_factor + jnp.sum(forward_weights, axis=-1)
        weights_low = forward_weights.astype(jnp.bfloat16)
        new_output = forward_output_sum * decay_factor[..., None] + jnp.einsum(
            "nts,snd->ntd", weights_low, value_block, preferred_element_type=jnp.float32
        )
        state = (new_max, new_sum, new_output)
        stored_blocks.append((key_block, value_block, pair_mask))
    row_max, row_sum, output_sum = state
    log_total = row_max + jnp.log(row_sum)
    attn_heads = (output_sum / row_sum[..., None]).astype(jnp.bfloat16).transpose(1, 0, 2)
    attention = attn_heads.reshape(tok_rows, feature_width)
    grad_full = lax.all_gather(grad_out, "fsdp", axis=1, tiled=True)
    grad_attn = lax.dot_general(
        grad_full,
        lax.all_gather(out_weight, "ctx", axis=0, tiled=True),
        (((1,), (1,)), ((), ())),
        preferred_element_type=jnp.float32,
    ).astype(jnp.bfloat16)
    grad_weight = lax.psum_scatter(
        lax.dot_general(
            attention, grad_full, (((0,), (0,)), ((), ())), preferred_element_type=jnp.float32
        ),
        "ctx",
        scatter_dimension=0,
        tiled=True,
    )
    grad_heads = grad_attn.reshape(tok_rows, head_count, DH)
    delta_sum = jnp.einsum(
        "tnd,tnd->nt", grad_heads, attn_heads, preferred_element_type=jnp.float32
    )
    grad_query = jnp.zeros((tok_rows, head_count, DH), jnp.float32)
    carried = None
    for cycle_step in range(cycle_reach + 1):
        key_block, value_block, pair_mask = stored_blocks[cycle_step]
        if cycle_step > 0:
            carried = jax.tree.map(
                lambda part, own: part.astype(own.dtype),
                passed_along(as_sent(carried), "ctx", 1),
                carried,
            )
        scores = scores_of(query_heads, key_block)
        weights = jnp.where(pair_mask[None], jnp.exp(scores - log_total[..., None]), 0.0)
        rounded = weights.astype(jnp.bfloat16)
        value_part = jnp.einsum(
            "nts,tnd->snd", rounded, grad_heads, preferred_element_type=jnp.float32
        )
        grad_weights = jnp.einsum(
            "tnd,snd->nts", grad_heads, value_block, preferred_element_type=jnp.float32
        )
        grad_scores = (weights * (grad_weights - delta_sum[..., None])).astype(jnp.bfloat16)
        query_part = (
            jnp.einsum("nts,snd->tnd", grad_scores, key_block, preferred_element_type=jnp.float32)
            * score_scale
        )
        key_part = (
            jnp.einsum("nts,tnd->snd", grad_scores, query_heads, preferred_element_type=jnp.float32)
            * score_scale
        )
        query_part, key_part, value_part = (query_part, key_part, value_part)
        grad_query = grad_query + query_part
        if cycle_step == 0:
            carried = (key_part, value_part)
        else:
            carried = (carried[0] + key_part, carried[1] + value_part)
    grad_key, grad_value = jax.tree.map(
        lambda part, own: part.astype(own.dtype),
        passed_along(as_sent(carried), "ctx", -cycle_reach),
        carried,
    )
    return (
        grad_query.reshape(tok_rows, feature_width).astype(jnp.bfloat16),
        grad_key.reshape(tok_rows, feature_width).astype(jnp.bfloat16),
        grad_value.reshape(tok_rows, feature_width).astype(jnp.bfloat16),
        grad_weight,
    )


def solution(mesh):
    return jax.shard_map(
        shards,
        mesh=mesh,
        in_specs=(
            P("ctx", "fsdp"),
            P("ctx", "fsdp"),
            P("ctx", "fsdp"),
            P("ctx"),
            P(("fsdp", "ctx"), None),
            P("ctx", "fsdp"),
        ),
        out_specs=(P("ctx", "fsdp"), P("ctx", "fsdp"), P("ctx", "fsdp"), P(("fsdp", "ctx"), None)),
        check_vma=False,
    )
```

profile of v0, /device:TPU:8, one launch (start us, length us, event | category | flops | bytes accessed | tf_op | source)
XLA Modules:
  0.0 712.0 jit_solution(2859584681869793939)
XLA Ops:
  9.4 3.4 collective-permute-start
  12.8 8.0 %collective-permute-done = s32[256]{0:T(256)S(1)} collective-permute-done((s32[256]{0:T(256)S(1)}, s32[256]{0:T(256)S(1)}, u32[]{:S(2)}, u32[]{:S(2)}) %collective-permute-start) | collective-permute-done | bytes 1056 | tf_op jit(solution)/shard_map/ppermute | solution.py:17
  22.7 7.8 %collective-permute-done.2 = s32[256]{0:T(256)S(1)} collective-permute-done((s32[256]{0:T(256)S(1)}, s32[256]{0:T(256)S(1)}, u32[]{:S(2)}, u32[]{:S(2)}) %collective-permute-start.2) | collective-permute-done | bytes 1056 | tf_op jit(solution)/shard_map/ppermute | solution.py:17
  33.6 1.9 collective-permute-start.1
  36.7 1.9 collective-permute-start.16
  42.1 9.6 %collective-permute-done.6 = s32[256]{0:T(256)S(1)} collective-permute-done((s32[256]{0:T(256)S(1)}, s32[256]{0:T(256)S(1)}, u32[]{:S(2)}, u32[]{:S(2)}) %collective-permute-start.6) | collective-permute-done | bytes 1056 | tf_op jit(solution)/shard_map/ppermute | solution.py:17
  53.6 7.7 %collective-permute-done.8 = s32[256]{0:T(256)S(1)} collective-permute-done((s32[256]{0:T(256)S(1)}, s32[256]{0:T(256)S(1)}, u32[]{:S(2)}, u32[]{:S(2)}) %collective-permute-start.8) | collective-permute-done | bytes 1056 | tf_op jit(solution)/shard_map/ppermute | solution.py:17
  63.3 7.8 %collective-permute-done.10 = s32[256]{0:T(256)S(1)} collective-permute-done((s32[256]{0:T(256)S(1)}, s32[256]{0:T(256)S(1)}, u32[]{:S(2)}, u32[]{:S(2)}) %collective-permute-start.10) | collective-permute-done | bytes 1056 | tf_op jit(solution)/shard_map/ppermute | solution.py:17
  73.0 7.7 %collective-permute-done.12 = s32[256]{0:T(256)S(1)} collective-permute-done((s32[256]{0:T(256)S(1)}, s32[256]{0:T(256)S(1)}, u32[]{:S(2)}, u32[]{:S(2)}) %collective-permute-start.12) | collective-permute-done | bytes 1056 | tf_op jit(solution)/shard_map/ppermute | solution.py:17
  82.6 7.7 %collective-permute-done.14 = s32[256]{0:T(256)S(1)} collective-permute-done((s32[256]{0:T(256)S(1)}, s32[256]{0:T(256)S(1)}, u32[]{:S(2)}, u32[]{:S(2)}) %collective-permute-start.14) | collective-permute-done | bytes 1056 | tf_op jit(solution)/shard_map/ppermute | solution.py:17
  93.6 1.9 collective-permute-start.17
  95.9 9.4 %collective-permute-done.3 = bf16[256,4,128]{2,0,1:T(8,128)(2,1)S(1)} collective-permute-done((bf16[256,4,128]{2,0,1:T(8,128)(2,1)S(1)}, bf16[256,4,128]{2,0,1:T(8,128)(2,1)S(1)}, u32[]{:S(2)}, u32[]{:S(2)}) %collective-permute-start.3) | collective-permute-done | bytes 262176 | tf_op jit(solution)/shard_map/ppermute | solution.py:17
  107.2 4.2 collective-permute-done.17
  113.7 4.8 collective-permute-done.5
  120.5 7.6 %collective-permute-done.18 = bf16[256,4,128]{0,2,1:T(8,128)(2,1)S(1)} collective-permute-done((bf16[256,4,128]{0,2,1:T(8,128)(2,1)S(1)}, bf16[256,4,128]{0,2,1:T(8,128)(2,1)S(1)}, u32[]{:S(2)}, u32[]{:S(2)}) %collective-permute-start.18) | collective-permute-done | bytes 262176 | tf_op jit(solution)/shard_map/ppermute | solution.py:17
  130.3 3.6 collective-permute-done.7
  135.9 6.3 collective-permute-done.19
  144.5 4.9 collective-permute-done.9
  151.3 3.9 collective-permute-done.20
  157.4 7.1 %collective-permute-done.11 = bf16[256,4,128]{2,0,1:T(8,128)(2,1)S(1)} collective-permute-done((bf16[256,4,128]{2,0,1:T(8,128)(2,1)S(1)}, bf16[256,4,128]{2,0,1:T(8,128)(2,1)S(1)}, u32[]{:S(2)}, u32[]{:S(2)}) %collective-permute-start.11) | collective-permute-done | bytes 262176 | tf_op jit(solution)/shard_map/ppermute | solution.py:17
  166.5 4.0 collective-permute-done.21
  172.7 6.6 collective-permute-done.13
  181.3 5.6 collective-permute-done.22
  186.9 2.4 collective-permute-start.23
  189.6 2.4 collective-permute-done.15
  198.8 2.2 fusion.33
  201.0 145.4 %all-gather.5.cloned.1.call-done = bf16[512,4096]{1,0:T(8,128)(2,1)} async-done(((bf16[8,4096]{1,0:T(8,128)(2,1)}), bf16[512,4096]{1,0:T(8,128)(2,1)}) %all-gather.5.cloned.1.call-update) | async-done | bytes 4194320 | tf_op jit(solution)/shard_map/all_gather | solution.py:92
  346.4 4.8 convolution_convert_fusion.1
  354.8 2.1 copy.235
  358.9 4.6 fusion.291
  379.5 2.3 collective-permute-done.24
  382.2 6.9 collective-permute-done.33
  389.9 8.2 %collective-permute-done.25 = bf16[256,4,128]{0,2,1:T(8,128)(2,1)S(1)} collective-permute-done((bf16[256,4,128]{0,2,1:T(8,128)(2,1)S(1)}, bf16[256,4,128]{0,2,1:T(8,128)(2,1)S(1)}, u32[]{:S(2)}, u32[]{:S(2)}) %collective-permute-start.25) | collective-permute-done | bytes 262176 | tf_op jit(solution)/shard_map/ppermute | solution.py:31
  398.2 8.1 %collective-permute-done.34 = bf16[256,4,128]{0,2,1:T(8,128)(2,1)S(1)} collective-permute-done((bf16[256,4,128]{0,2,1:T(8,128)(2,1)S(1)}, bf16[256,4,128]{0,2,1:T(8,128)(2,1)S(1)}, u32[]{:S(2)}, u32[]{:S(2)}) %collective-permute-start.34) | collective-permute-done | bytes 262176 | tf_op jit(solution)/shard_map/ppermute | solution.py:31
  407.1 6.8 collective-permute-done.26
  414.0 7.5 %collective-permute-done.35 = bf16[256,4,128]{0,2,1:T(8,128)(2,1)S(1)} collective-permute-done((bf16[256,4,128]{0,2,1:T(8,128)(2,1)S(1)}, bf16[256,4,128]{0,2,1:T(8,128)(2,1)S(1)}, u32[]{:S(2)}, u32[]{:S(2)}) %collective-permute-start.35) | collective-permute-done | bytes 262176 | tf_op jit(solution)/shard_map/ppermute | solution.py:31
  422.3 6.5 collective-permute-done.27
  429.2 3.8 collective-permute-done.36
  433.8 7.6 %collective-permute-done.28 = bf16[256,4,128]{0,2,1:T(8,128)(2,1)S(1)} collective-permute-done((bf16[256,4,128]{0,2,1:T(8,128)(2,1)S(1)}, bf16[256,4,128]{0,2,1:T(8,128)(2,1)S(1)}, u32[]{:S(2)}, u32[]{:S(2)}) %collective-permute-start.28) | collective-permute-done | bytes 262176 | tf_op jit(solution)/shard_map/ppermute | solution.py:31
  441.5 3.4 collective-permute-done.37
  445.7 7.2 %collective-permute-done.29 = bf16[256,4,128]{0,2,1:T(8,128)(2,1)S(1)} collective-permute-done((bf16[256,4,128]{0,2,1:T(8,128)(2,1)S(1)}, bf16[256,4,128]{0,2,1:T(8,128)(2,1)S(1)}, u32[]{:S(2)}, u32[]{:S(2)}) %collective-permute-start.29) | collective-permute-done | bytes 262176 | tf_op jit(solution)/shard_map/ppermute | solution.py:31
  453.1 4.0 collective-permute-done.38
  457.8 6.4 collective-permute-done.30
  464.4 5.0 collective-permute-done.39
  470.2 5.6 collective-permute-done.31
  475.9 5.7 collective-permute-done.40
  484.6 6.3 collective-permute-done.41
  491.8 213.5 %reduce-scatter.2.cloned.1.call-done = f32[8,4096]{1,0:T(8,128)} async-done(((f32[512,4096]{1,0:T(8,128)}), f32[8,4096]{1,0:T(8,128)}) %reduce-scatter.2.cloned.1.call-update) | async-done | bytes 131088 | tf_op jit(solution)/shard_map/reduce_scatter | solution.py:96
  (328 shorter events, 83.8 us)
Async XLA Ops:
  7.2 193.8 %all-gather.3.cloned.1.call-start = ((), (), s32[]{:S(2)}) async-start(), calls=%async_computation.1 | async-start | bytes 2621440 | tf_op jit(solution)/shard_map/all_gather | solution.py:89
  7.9 338.5 %all-gather.5.cloned.1.call-start = ((), (), s32[]{:S(2)}) async-start(), calls=%async_computation.2 | async-start | bytes 4259840 | tf_op jit(solution)/shard_map/all_gather | solution.py:92
  8.7 696.6 %reduce-scatter.2.cloned.1.call-start = ((), (), s32[]{:S(2)}) async-start(), calls=%async_computation.3 | async-start | bytes 8519680 | tf_op jit(solution)/shard_map/reduce_scatter | solution.py:96
  9.4 11.4 %collective-permute-start = (s32[256]{0:T(256)S(1)}, s32[256]{0:T(256)S(1)}, u32[]{:S(2)}, u32[]{:S(2)}) collective-permute-start(s32[256]{0:T(256)S(1)} %broadcast_add_fusion), channel_id=1, source_target_pairs={{0,4},{4,8},{8,12},{12,16},{16,20},{20,24},{24,28},{28,32},{32,36}... | collective-permute-start | bytes 3080 | tf_op jit(solution)/shard_map/ppermute | solution.py:17
  20.8 9.7 %collective-permute-start.2 = (s32[256]{0:T(256)S(1)}, s32[256]{0:T(256)S(1)}, u32[]{:S(2)}, u32[]{:S(2)}) collective-permute-start(s32[256]{0:T(256)S(1)} %collective-permute-done), channel_id=1, source_target_pairs={{0,4},{4,8},{8,12},{12,16},{16,20},{20,24},{24,28},{28,32},{32,36}... | collective-permute-start | bytes 3080 | tf_op jit(solution)/shard_map/ppermute | solution.py:17
  30.5 9.7 %collective-permute-start.4 = (s32[256]{0:T(256)S(1)}, s32[256]{0:T(256)S(1)}, u32[]{:S(2)}, u32[]{:S(2)}) collective-permute-start(s32[256]{0:T(256)S(1)} %collective-permute-done.2), channel_id=1, source_target_pairs={{0,4},{4,8},{8,12},{12,16},{16,20},{20,24},{24,28},{28,32},{32,36}... | collective-permute-start | bytes 3080 | tf_op jit(solution)/shard_map/ppermute | solution.py:17
  33.6 58.0 %collective-permute-start.1 = (bf16[256,4,128]{2,0,1:T(8,128)(2,1)S(1)}, bf16[256,4,128]{2,0,1:T(8,128)(2,1)S(1)}, u32[]{:S(2)}, u32[]{:S(2)}) collective-permute-start(bf16[256,4,128]{2,0,1:T(8,128)(2,1)S(1)} %copy.116), channel_id=1, source_target_pairs={{0,4},{4,8},{8,12},{12,16},{16,20},{20,24},{24,28},{28,32},{32,36}... | collective-permute-start | bytes 786440 | tf_op jit(solution)/shard_map/ppermute | solution.py:17
  36.7 56.9 %collective-permute-start.16 = (bf16[256,4,128]{0,2,1:T(8,128)(2,1)S(1)}, bf16[256,4,128]{0,2,1:T(8,128)(2,1)S(1)}, u32[]{:S(2)}, u32[]{:S(2)}) collective-permute-start(bf16[256,4,128]{0,2,1:T(8,128)(2,1)S(1)} %bitcast.466), channel_id=1, source_target_pairs={{0,4},{4,8},{8,12},{12,16},{16,20},{20,24},{24,28},{28,32},{32,36}... | collective-permute-start | bytes 786440 | tf_op jit(solution)/shard_map/ppermute | solution.py:17
  40.1 11.6 %collective-permute-start.6 = (s32[256]{0:T(256)S(1)}, s32[256]{0:T(256)S(1)}, u32[]{:S(2)}, u32[]{:S(2)}) collective-permute-start(s32[256]{0:T(256)S(1)} %collective-permute-done.4), channel_id=1, source_target_pairs={{0,4},{4,8},{8,12},{12,16},{16,20},{20,24},{24,28},{28,32},{32,36}... | collective-permute-start | bytes 3080 | tf_op jit(solution)/shard_map/ppermute | solution.py:17
  51.7 9.7 %collective-permute-start.8 = (s32[256]{0:T(256)S(1)}, s32[256]{0:T(256)S(1)}, u32[]{:S(2)}, u32[]{:S(2)}) collective-permute-start(s32[256]{0:T(256)S(1)} %collective-permute-done.6), channel_id=1, source_target_pairs={{0,4},{4,8},{8,12},{12,16},{16,20},{20,24},{24,28},{28,32},{32,36}... | collective-permute-start | bytes 3080 | tf_op jit(solution)/shard_map/ppermute | solution.py:17
  61.4 9.7 %collective-permute-start.10 = (s32[256]{0:T(256)S(1)}, s32[256]{0:T(256)S(1)}, u32[]{:S(2)}, u32[]{:S(2)}) collective-permute-start(s32[256]{0:T(256)S(1)} %collective-permute-done.8), channel_id=1, source_target_pairs={{0,4},{4,8},{8,12},{12,16},{16,20},{20,24},{24,28},{28,32},{32,36}... | collective-permute-start | bytes 3080 | tf_op jit(solution)/shard_map/ppermute | solution.py:17
  71.0 9.7 %collective-permute-start.12 = (s32[256]{0:T(256)S(1)}, s32[256]{0:T(256)S(1)}, u32[]{:S(2)}, u32[]{:S(2)}) collective-permute-start(s32[256]{0:T(256)S(1)} %collective-permute-done.10), channel_id=1, source_target_pairs={{0,4},{4,8},{8,12},{12,16},{16,20},{20,24},{24,28},{28,32},{32,36}... | collective-permute-start | bytes 3080 | tf_op jit(solution)/shard_map/ppermute | solution.py:17
  80.7 9.7 %collective-permute-start.14 = (s32[256]{0:T(256)S(1)}, s32[256]{0:T(256)S(1)}, u32[]{:S(2)}, u32[]{:S(2)}) collective-permute-start(s32[256]{0:T(256)S(1)} %collective-permute-done.12), channel_id=1, source_target_pairs={{0,4},{4,8},{8,12},{12,16},{16,20},{20,24},{24,28},{28,32},{32,36}... | collective-permute-start | bytes 3080 | tf_op jit(solution)/shard_map/ppermute | solution.py:17
  91.2 106.7 %copy-start.21 = (pred[256,256]{0,1:T(8,128)(4,1)}, pred[256,256]{0,1:T(8,128)(4,1)S(1)}, u32[]{:S(2)}) copy-start(pred[256,256]{0,1:T(8,128)(4,1)S(1)} %get-tuple-element.36) | copy-start | bytes 196612
  91.3 107.1 %copy-start.19 = (pred[256,256]{0,1:T(8,128)(4,1)}, pred[256,256]{0,1:T(8,128)(4,1)S(1)}, u32[]{:S(2)}) copy-start(pred[256,256]{0,1:T(8,128)(4,1)S(1)} %get-tuple-element.37) | copy-start | bytes 196612
  91.7 13.6 %collective-permute-start.3 = (bf16[256,4,128]{2,0,1:T(8,128)(2,1)S(1)}, bf16[256,4,128]{2,0,1:T(8,128)(2,1)S(1)}, u32[]{:S(2)}, u32[]{:S(2)}) collective-permute-start(bf16[256,4,128]{2,0,1:T(8,128)(2,1)S(1)} %collective-permute-done.1), channel_id=1, source_target_pairs={{0,4},{4,8},{8,12},{12,16},{16,20},{20,24},{24,28},{28,32},{32,36}... | collective-permute-start | bytes 786440 | tf_op jit(solution)/shard_map/ppermute | solution.py:17
  93.6 17.8 %collective-permute-start.17 = (bf16[256,4,128]{0,2,1:T(8,128)(2,1)S(1)}, bf16[256,4,128]{0,2,1:T(8,128)(2,1)S(1)}, u32[]{:S(2)}, u32[]{:S(2)}) collective-permute-start(bf16[256,4,128]{0,2,1:T(8,128)(2,1)S(1)} %collective-permute-done.16), channel_id=1, source_target_pairs={{0,4},{4,8},{8,12},{12,16},{16,20},{20,24},{24,28},{28,32},{32,36}... | collective-permute-start | bytes 786440 | tf_op jit(solution)/shard_map/ppermute | solution.py:17
  105.3 13.3 %collective-permute-start.5 = (bf16[256,4,128]{2,0,1:T(8,128)(2,1)S(1)}, bf16[256,4,128]{2,0,1:T(8,128)(2,1)S(1)}, u32[]{:S(2)}, u32[]{:S(2)}) collective-permute-start(bf16[256,4,128]{2,0,1:T(8,128)(2,1)S(1)} %collective-permute-done.3), channel_id=1, source_target_pairs={{0,4},{4,8},{8,12},{12,16},{16,20},{20,24},{24,28},{28,32},{32,36}... | collective-permute-start | bytes 786440 | tf_op jit(solution)/shard_map/ppermute | solution.py:17
  111.4 16.6 %collective-permute-start.18 = (bf16[256,4,128]{0,2,1:T(8,128)(2,1)S(1)}, bf16[256,4,128]{0,2,1:T(8,128)(2,1)S(1)}, u32[]{:S(2)}, u32[]{:S(2)}) collective-permute-start(bf16[256,4,128]{0,2,1:T(8,128)(2,1)S(1)} %collective-permute-done.17), channel_id=1, source_target_pairs={{0,4},{4,8},{8,12},{12,16},{16,20},{20,24},{24,28},{28,32},{32,36}... | collective-permute-start | bytes 786440 | tf_op jit(solution)/shard_map/ppermute | solution.py:17
  118.6 15.4 %collective-permute-start.7 = (bf16[256,4,128]{2,0,1:T(8,128)(2,1)S(1)}, bf16[256,4,128]{2,0,1:T(8,128)(2,1)S(1)}, u32[]{:S(2)}, u32[]{:S(2)}) collective-permute-start(bf16[256,4,128]{2,0,1:T(8,128)(2,1)S(1)} %collective-permute-done.5), channel_id=1, source_target_pairs={{0,4},{4,8},{8,12},{12,16},{16,20},{20,24},{24,28},{28,32},{32,36}... | collective-permute-start | bytes 786440 | tf_op jit(solution)/shard_map/ppermute | solution.py:17
  128.0 14.1 %collective-permute-start.19 = (bf16[256,4,128]{0,2,1:T(8,128)(2,1)S(1)}, bf16[256,4,128]{0,2,1:T(8,128)(2,1)S(1)}, u32[]{:S(2)}, u32[]{:S(2)}) collective-permute-start(bf16[256,4,128]{0,2,1:T(8,128)(2,1)S(1)} %collective-permute-done.18), channel_id=1, source_target_pairs={{0,4},{4,8},{8,12},{12,16},{16,20},{20,24},{24,28},{28,32},{32,36}... | collective-permute-start | bytes 786440 | tf_op jit(solution)/shard_map/ppermute | solution.py:17
  134.0 15.4 %collective-permute-start.9 = (bf16[256,4,128]{2,0,1:T(8,128)(2,1)S(1)}, bf16[256,4,128]{2,0,1:T(8,128)(2,1)S(1)}, u32[]{:S(2)}, u32[]{:S(2)}) collective-permute-start(bf16[256,4,128]{2,0,1:T(8,128)(2,1)S(1)} %collective-permute-done.7), channel_id=1, source_target_pairs={{0,4},{4,8},{8,12},{12,16},{16,20},{20,24},{24,28},{28,32},{32,36}... | collective-permute-start | bytes 786440 | tf_op jit(solution)/shard_map/ppermute | solution.py:17
  142.2 13.0 %collective-permute-start.20 = (bf16[256,4,128]{0,2,1:T(8,128)(2,1)S(1)}, bf16[256,4,128]{0,2,1:T(8,128)(2,1)S(1)}, u32[]{:S(2)}, u32[]{:S(2)}) collective-permute-start(bf16[256,4,128]{0,2,1:T(8,128)(2,1)S(1)} %collective-permute-done.19), channel_id=1, source_target_pairs={{0,4},{4,8},{8,12},{12,16},{16,20},{20,24},{24,28},{28,32},{32,36}... | collective-permute-start | bytes 786440 | tf_op jit(solution)/shard_map/ppermute | solution.py:17
  149.3 15.2 %collective-permute-start.11 = (bf16[256,4,128]{2,0,1:T(8,128)(2,1)S(1)}, bf16[256,4,128]{2,0,1:T(8,128)(2,1)S(1)}, u32[]{:S(2)}, u32[]{:S(2)}) collective-permute-start(bf16[256,4,128]{2,0,1:T(8,128)(2,1)S(1)} %collective-permute-done.9), channel_id=1, source_target_pairs={{0,4},{4,8},{8,12},{12,16},{16,20},{20,24},{24,28},{28,32},{32,36}... | collective-permute-start | bytes 786440 | tf_op jit(solution)/shard_map/ppermute | solution.py:17
  155.2 15.3 %collective-permute-start.21 = (bf16[256,4,128]{0,2,1:T(8,128)(2,1)S(1)}, bf16[256,4,128]{0,2,1:T(8,128)(2,1)S(1)}, u32[]{:S(2)}, u32[]{:S(2)}) collective-permute-start(bf16[256,4,128]{0,2,1:T(8,128)(2,1)S(1)} %collective-permute-done.20), channel_id=1, source_target_pairs={{0,4},{4,8},{8,12},{12,16},{16,20},{20,24},{24,28},{28,32},{32,36}... | collective-permute-start | bytes 786440 | tf_op jit(solution)/shard_map/ppermute | solution.py:17
  164.6 14.8 %collective-permute-start.13 = (bf16[256,4,128]{2,0,1:T(8,128)(2,1)S(1)}, bf16[256,4,128]{2,0,1:T(8,128)(2,1)S(1)}, u32[]{:S(2)}, u32[]{:S(2)}) collective-permute-start(bf16[256,4,128]{2,0,1:T(8,128)(2,1)S(1)} %collective-permute-done.11), channel_id=1, source_target_pairs={{0,4},{4,8},{8,12},{12,16},{16,20},{20,24},{24,28},{28,32},{32,36}... | collective-permute-start | bytes 786440 | tf_op jit(solution)/shard_map/ppermute | solution.py:17
  170.5 16.4 %collective-permute-start.22 = (bf16[256,4,128]{0,2,1:T(8,128)(2,1)S(1)}, bf16[256,4,128]{0,2,1:T(8,128)(2,1)}, u32[]{:S(2)}, u32[]{:S(2)}) collective-permute-start(bf16[256,4,128]{0,2,1:T(8,128)(2,1)S(1)} %collective-permute-done.21), channel_id=1, source_target_pairs={{0,4},{4,8},{8,12},{12,16},{16,20},{20,24},{24,28},{28,32},{32,36}... | collective-permute-start | bytes 786440 | tf_op jit(solution)/shard_map/ppermute | solution.py:17
  179.3 12.6 %collective-permute-start.15 = (bf16[256,4,128]{2,0,1:T(8,128)(2,1)S(1)}, bf16[256,4,128]{2,0,1:T(8,128)(2,1)S(1)}, u32[]{:S(2)}, u32[]{:S(2)}) collective-permute-start(bf16[256,4,128]{2,0,1:T(8,128)(2,1)S(1)} %collective-permute-done.13), channel_id=1, source_target_pairs={{0,4},{4,8},{8,12},{12,16},{16,20},{20,24},{24,28},{28,32},{32,36}... | collective-permute-start | bytes 786440 | tf_op jit(solution)/shard_map/ppermute | solution.py:17
  186.9 169.9 %collective-permute-start.23 = (bf16[256,4,128]{0,2,1:T(8,128)(2,1)}, bf16[256,4,128]{0,2,1:T(8,128)(2,1)}, u32[]{:S(2)}, u32[]{:S(2)}) collective-permute-start(bf16[256,4,128]{0,2,1:T(8,128)(2,1)} %collective-permute-done.22), channel_id=1, source_target_pairs={{0,4},{4,8},{8,12},{12,16},{16,20},{20,24},{24,28},{28,32},{32,36}... | collective-permute-start | bytes 786440 | tf_op jit(solution)/shard_map/ppermute | solution.py:17
  192.3 164.5 %copy-start.13 = (f32[4,256,256]{1,2,0:T(8,128)}, f32[4,256,256]{1,2,0:T(8,128)S(1)}, u32[]{:S(2)}) copy-start(f32[4,256,256]{1,2,0:T(8,128)S(1)} %get-tuple-element.43) | copy-start | bytes 3145732
  366.9 14.9 %collective-permute-start.24 = (bf16[256,4,128]{0,2,1:T(8,128)(2,1)S(1)}, bf16[256,4,128]{0,2,1:T(8,128)(2,1)S(1)}, u32[]{:S(2)}, u32[]{:S(2)}) collective-permute-start(bf16[256,4,128]{0,2,1:T(8,128)(2,1)S(1)} %fusion.49), channel_id=1, source_target_pairs={{252,0},{0,4},{4,8},{8,12},{12,16},{16,20},{20,24},{24,28},{28,32}... | collective-permute-start | bytes 786440 | tf_op jit(solution)/shard_map/ppermute | solution.py:31
  367.6 21.5 %collective-permute-start.33 = (bf16[256,4,128]{0,2,1:T(8,128)(2,1)S(1)}, bf16[256,4,128]{0,2,1:T(8,128)(2,1)S(1)}, u32[]{:S(2)}, u32[]{:S(2)}) collective-permute-start(bf16[256,4,128]{0,2,1:T(8,128)(2,1)S(1)} %fusion.48), channel_id=1, source_target_pairs={{252,0},{0,4},{4,8},{8,12},{12,16},{16,20},{20,24},{24,28},{28,32}... | collective-permute-start | bytes 786440 | tf_op jit(solution)/shard_map/ppermute | solution.py:31
  382.1 16.0 %collective-permute-start.25 = (bf16[256,4,128]{0,2,1:T(8,128)(2,1)S(1)}, bf16[256,4,128]{0,2,1:T(8,128)(2,1)S(1)}, u32[]{:S(2)}, u32[]{:S(2)}) collective-permute-start(bf16[256,4,128]{0,2,1:T(8,128)(2,1)S(1)} %add_convert_fusion.8), channel_id=1, source_target_pairs={{252,0},{0,4},{4,8},{8,12},{12,16},{16,20},{20,24},{24,28},{28,32}... | collective-permute-start | bytes 786440 | tf_op jit(solution)/shard_map/ppermute | solution.py:31
  389.5 16.9 %collective-permute-start.34 = (bf16[256,4,128]{0,2,1:T(8,128)(2,1)S(1)}, bf16[256,4,128]{0,2,1:T(8,128)(2,1)S(1)}, u32[]{:S(2)}, u32[]{:S(2)}) collective-permute-start(bf16[256,4,128]{0,2,1:T(8,128)(2,1)S(1)} %add_convert_fusion), channel_id=1, source_target_pairs={{252,0},{0,4},{4,8},{8,12},{12,16},{16,20},{20,24},{24,28},{28,32}... | collective-permute-start | bytes 786440 | tf_op jit(solution)/shard_map/ppermute | solution.py:31
  398.2 15.7 %collective-permute-start.26 = (bf16[256,4,128]{0,2,1:T(8,128)(2,1)S(1)}, bf16[256,4,128]{0,2,1:T(8,128)(2,1)S(1)}, u32[]{:S(2)}, u32[]{:S(2)}) collective-permute-start(bf16[256,4,128]{0,2,1:T(8,128)(2,1)S(1)} %add_convert_fusion.7), channel_id=1, source_target_pairs={{252,0},{0,4},{4,8},{8,12},{12,16},{16,20},{20,24},{24,28},{28,32}... | collective-permute-start | bytes 786440 | tf_op jit(solution)/shard_map/ppermute | solution.py:31
  406.7 14.9 %collective-permute-start.35 = (bf16[256,4,128]{0,2,1:T(8,128)(2,1)S(1)}, bf16[256,4,128]{0,2,1:T(8,128)(2,1)S(1)}, u32[]{:S(2)}, u32[]{:S(2)}) collective-permute-start(bf16[256,4,128]{0,2,1:T(8,128)(2,1)S(1)} %fusion.132), channel_id=1, source_target_pairs={{252,0},{0,4},{4,8},{8,12},{12,16},{16,20},{20,24},{24,28},{28,32}... | collective-permute-start | bytes 786440 | tf_op jit(solution)/shard_map/ppermute | solution.py:31
  413.9 14.9 %collective-permute-start.27 = (bf16[256,4,128]{0,2,1:T(8,128)(2,1)S(1)}, bf16[256,4,128]{0,2,1:T(8,128)(2,1)S(1)}, u32[]{:S(2)}, u32[]{:S(2)}) collective-permute-start(bf16[256,4,128]{0,2,1:T(8,128)(2,1)S(1)} %add_convert_fusion.6), channel_id=1, source_target_pairs={{252,0},{0,4},{4,8},{8,12},{12,16},{16,20},{20,24},{24,28},{28,32}... | collective-permute-start | bytes 786440 | tf_op jit(solution)/shard_map/ppermute | solution.py:31
  421.9 11.1 %collective-permute-start.36 = (bf16[256,4,128]{0,2,1:T(8,128)(2,1)S(1)}, bf16[256,4,128]{0,2,1:T(8,128)(2,1)S(1)}, u32[]{:S(2)}, u32[]{:S(2)}) collective-permute-start(bf16[256,4,128]{0,2,1:T(8,128)(2,1)S(1)} %fusion.125), channel_id=1, source_target_pairs={{252,0},{0,4},{4,8},{8,12},{12,16},{16,20},{20,24},{24,28},{28,32}... | collective-permute-start | bytes 786440 | tf_op jit(solution)/shard_map/ppermute | solution.py:31
  428.9 12.5 %collective-permute-start.28 = (bf16[256,4,128]{0,2,1:T(8,128)(2,1)S(1)}, bf16[256,4,128]{0,2,1:T(8,128)(2,1)S(1)}, u32[]{:S(2)}, u32[]{:S(2)}) collective-permute-start(bf16[256,4,128]{0,2,1:T(8,128)(2,1)S(1)} %add_convert_fusion.5), channel_id=1, source_target_pairs={{252,0},{0,4},{4,8},{8,12},{12,16},{16,20},{20,24},{24,28},{28,32}... | collective-permute-start | bytes 786440 | tf_op jit(solution)/shard_map/ppermute | solution.py:31
  433.4 11.6 %collective-permute-start.37 = (bf16[256,4,128]{0,2,1:T(8,128)(2,1)S(1)}, bf16[256,4,128]{0,2,1:T(8,128)(2,1)S(1)}, u32[]{:S(2)}, u32[]{:S(2)}) collective-permute-start(bf16[256,4,128]{0,2,1:T(8,128)(2,1)S(1)} %fusion.118), channel_id=1, source_target_pairs={{252,0},{0,4},{4,8},{8,12},{12,16},{16,20},{20,24},{24,28},{28,32}... | collective-permute-start | bytes 786440 | tf_op jit(solution)/shard_map/ppermute | solution.py:31
  441.4 11.5 %collective-permute-start.29 = (bf16[256,4,128]{0,2,1:T(8,128)(2,1)S(1)}, bf16[256,4,128]{0,2,1:T(8,128)(2,1)S(1)}, u32[]{:S(2)}, u32[]{:S(2)}) collective-permute-start(bf16[256,4,128]{0,2,1:T(8,128)(2,1)S(1)} %add_convert_fusion.4), channel_id=1, source_target_pairs={{252,0},{0,4},{4,8},{8,12},{12,16},{16,20},{20,24},{24,28},{28,32}... | collective-permute-start | bytes 786440 | tf_op jit(solution)/shard_map/ppermute | solution.py:31
  445.3 11.7 %collective-permute-start.38 = (bf16[256,4,128]{0,2,1:T(8,128)(2,1)S(1)}, bf16[256,4,128]{0,2,1:T(8,128)(2,1)S(1)}, u32[]{:S(2)}, u32[]{:S(2)}) collective-permute-start(bf16[256,4,128]{0,2,1:T(8,128)(2,1)S(1)} %fusion.111), channel_id=1, source_target_pairs={{252,0},{0,4},{4,8},{8,12},{12,16},{16,20},{20,24},{24,28},{28,32}... | collective-permute-start | bytes 786440 | tf_op jit(solution)/shard_map/ppermute | solution.py:31
  453.0 11.2 %collective-permute-start.30 = (bf16[256,4,128]{0,2,1:T(8,128)(2,1)S(1)}, bf16[256,4,128]{0,2,1:T(8,128)(2,1)S(1)}, u32[]{:S(2)}, u32[]{:S(2)}) collective-permute-start(bf16[256,4,128]{0,2,1:T(8,128)(2,1)S(1)} %add_convert_fusion.3), channel_id=1, source_target_pairs={{252,0},{0,4},{4,8},{8,12},{12,16},{16,20},{20,24},{24,28},{28,32}... | collective-permute-start | bytes 786440 | tf_op jit(solution)/shard_map/ppermute | solution.py:31
  457.3 12.0 %collective-permute-start.39 = (bf16[256,4,128]{0,2,1:T(8,128)(2,1)S(1)}, bf16[256,4,128]{0,2,1:T(8,128)(2,1)S(1)}, u32[]{:S(2)}, u32[]{:S(2)}) collective-permute-start(bf16[256,4,128]{0,2,1:T(8,128)(2,1)S(1)} %fusion.104), channel_id=1, source_target_pairs={{252,0},{0,4},{4,8},{8,12},{12,16},{16,20},{20,24},{24,28},{28,32}... | collective-permute-start | bytes 786440 | tf_op jit(solution)/shard_map/ppermute | solution.py:31
  464.3 11.5 %collective-permute-start.31 = (bf16[256,4,128]{0,2,1:T(8,128)(2,1)S(1)}, bf16[256,4,128]{0,2,1:T(8,128)(2,1)S(1)}, u32[]{:S(2)}, u32[]{:S(2)}) collective-permute-start(bf16[256,4,128]{0,2,1:T(8,128)(2,1)S(1)} %add_convert_fusion.2), channel_id=1, source_target_pairs={{252,0},{0,4},{4,8},{8,12},{12,16},{16,20},{20,24},{24,28},{28,32}... | collective-permute-start | bytes 786440 | tf_op jit(solution)/shard_map/ppermute | solution.py:31
  469.7 11.9 %collective-permute-start.40 = (bf16[256,4,128]{0,2,1:T(8,128)(2,1)S(1)}, bf16[256,4,128]{0,2,1:T(8,128)(2,1)S(1)}, u32[]{:S(2)}, u32[]{:S(2)}) collective-permute-start(bf16[256,4,128]{0,2,1:T(8,128)(2,1)S(1)} %fusion.97), channel_id=1, source_target_pairs={{252,0},{0,4},{4,8},{8,12},{12,16},{16,20},{20,24},{24,28},{28,32}... | collective-permute-start | bytes 786440 | tf_op jit(solution)/shard_map/ppermute | solution.py:31
  475.8 7.9 %collective-permute-start.32 = (bf16[256,4,128]{0,2,1:T(8,128)(2,1)S(1)}, bf16[256,4,128]{0,2,1:T(8,128)(2,1)S(1)}, u32[]{:S(2)}, u32[]{:S(2)}) collective-permute-start(bf16[256,4,128]{0,2,1:T(8,128)(2,1)S(1)} %add_convert_fusion.1), channel_id=1, source_target_pairs={{32,0},{36,4},{40,8},{44,12},{48,16},{52,20},{56,24},{60,28},{64,3... | collective-permute-start | bytes 786440 | tf_op jit(solution)/shard_map/ppermute | solution.py:31
  482.0 8.9 %collective-permute-start.41 = (bf16[256,4,128]{0,2,1:T(8,128)(2,1)S(1)}, bf16[256,4,128]{0,2,1:T(8,128)(2,1)S(1)}, u32[]{:S(2)}, u32[]{:S(2)}) collective-permute-start(bf16[256,4,128]{0,2,1:T(8,128)(2,1)S(1)} %fusion.90), channel_id=1, source_target_pairs={{32,0},{36,4},{40,8},{44,12},{48,16},{52,20},{56,24},{60,28},{64,3... | collective-permute-start | bytes 786440 | tf_op jit(solution)/shard_map/ppermute | solution.py:31
  (92 other events, 1862.3 us)
Sparse Core Ops, SparseCore 0:
  9.8 31.1 all-gather.2
  42.8 303.5 all-gather.4
  363.8 341.4 reduce-scatter.1
where the time goes:
time: 717 us; the launch traced here: 712 us
  waiting for transfers between devices  591 us (82%)
  starting transfers between devices  51.4 us (7%)
  matrix products  34.5 us (5%)
  between operations  15.8 us (2%)
  local copies, waits for them, and re-layouts  13 us (2%)
    reduce_scatter x1, waiting for transfers between devices, shards(): lax.psum_scatter(lax.dot_general(attention, grad_full, (((0,), (0,)), (()...  214 us
    all_gather x1, waiting for transfers between devices, shards(): lax.all_gather(out_weight, 'ctx', axis=0, tiled=True)  145 us
    ppermute x24, waiting for transfers between devices, shifted(): return lax.ppermute(array, axis, pairs)  128 us
    ppermute x18, waiting for transfers between devices, passed_along(): return lax.ppermute(block, axis, route)  102 us
    ppermute x24, starting transfers between devices, shifted(): return lax.ppermute(array, axis, pairs)  47.8 us
  transfers between devices with their start and end apart: 45, of which 41 were waited for; matrix products, arithmetic and copies ran while one was open for 6% of the time, Pallas kernels for 0%

commit v1 on v0

v1 whole, which is shorter than its diff:
```python
import math

import jax
import jax.numpy as jnp
from jax import lax
from jax.sharding import Mesh
from jax.sharding import PartitionSpec as P

DH = 128

NEGATIVE = -1e30

CTX = ("cy", "cz", "cx")
FS = ("fy", "fc")
CTX_SPLIT = (2, 8, 4)


def shifted_by(array, devices, by):
    pairs = [(i, i + by) for i in range(devices) if 0 <= i + by < devices]
    return lax.ppermute(array, CTX, pairs)


def make_shards(devices):
    def shards(query, key, value, doc_ids, out_weight, grad_out):
        tok_rows = query.shape[0]
        feature_width = query.shape[1]
        head_count = feature_width // DH
        cycle_reach = max(devices // 8, 2)
        cycle_index = lax.axis_index(CTX)
        score_scale = 1.0 / math.sqrt(DH)
        local_pos = jnp.arange(tok_rows, dtype=jnp.int32)
        own_pos = cycle_index * tok_rows + local_pos
        own_docs = doc_ids + 1
        query_heads = query.reshape(tok_rows, head_count, DH)

        grad_full = lax.all_gather(grad_out, FS, axis=1, tiled=True)
        weight_rows = out_weight
        for axis in ("cx", "cz", "cy"):
            weight_rows = lax.all_gather(weight_rows, axis, axis=0, tiled=True)

        key_value = jnp.concatenate([key, value], axis=1)
        blocks = [(key, value, own_docs)]
        for cycle_step in range(1, cycle_reach + 1):
            got = shifted_by(key_value, devices, cycle_step)
            got_docs = shifted_by(own_docs, devices, cycle_step)
            blocks.append((got[:, :feature_width], got[:, feature_width:], got_docs))

        def scores_of(query_block, key_block):
            return (
                jnp.einsum("tnd,snd->nts", query_block, key_block, preferred_element_type=jnp.float32)
                * score_scale
            )

        state = (
            jnp.full((head_count, tok_rows), NEGATIVE, jnp.float32),
            jnp.zeros((head_count, tok_rows), jnp.float32),
            jnp.zeros((head_count, tok_rows, DH), jnp.float32),
        )
        stored_blocks = []
        for cycle_step in range(cycle_reach + 1):
            key_rows, value_rows, key_docs = blocks[cycle_step]
            key_block = key_rows.reshape(tok_rows, head_count, DH)
            value_block = value_rows.reshape(tok_rows, head_count, DH)
            key_pos = own_pos - cycle_step * tok_rows
            pair_mask = (own_docs[:, None] == key_docs[None, :]) & (
                key_pos[None, :] <= own_pos[:, None]
            )
            forward_row_max, forward_row_sum, forward_output_sum = state
            forward_scores = jnp.where(pair_mask[None], scores_of(query_heads, key_block), NEGATIVE)
            new_max = jnp.maximum(forward_row_max, jnp.max(forward_scores, axis=-1))
            decay_factor = jnp.exp(forward_row_max - new_max)
            forward_weights = jnp.where(
                pair_mask[None], jnp.exp(forward_scores - new_max[..., None]), 0.0
            )
            new_sum = forward_row_sum * decay_factor + jnp.sum(forward_weights, axis=-1)
            weights_low = forward_weights.astype(jnp.bfloat16)
            new_output = forward_output_sum * decay_factor[..., None] + jnp.einsum(
                "nts,snd->ntd", weights_low, value_block, preferred_element_type=jnp.float32
            )
            state = (new_max, new_sum, new_output)
            stored_blocks.append((key_block, value_block, pair_mask))
        row_max, row_sum, output_sum = state
        log_total = row_max + jnp.log(row_sum)
        attn_heads = (output_sum / row_sum[..., None]).astype(jnp.bfloat16).transpose(1, 0, 2)
        attention = attn_heads.reshape(tok_rows, feature_width)

        partial_weight = lax.dot_general(
            attention, grad_full, (((0,), (0,)), ((), ())), preferred_element_type=jnp.float32
        )
        rows_each = partial_weight.shape[0] // devices
        partial_weight = (
            partial_weight.reshape(*CTX_SPLIT, rows_each, partial_weight.shape[1])
            .transpose(1, 2, 0, 3, 4)
            .reshape(partial_weight.shape)
        )
        for axis in ("cz", "cx", "cy"):
            partial_weight = lax.psum_scatter(partial_weight, axis, scatter_dimension=0, tiled=True)
        grad_weight = partial_weight

        grad_attn = lax.dot_general(
            grad_full,
            weight_rows,
            (((1,), (1,)), ((), ())),
            preferred_element_type=jnp.float32,
        ).astype(jnp.bfloat16)
        grad_heads = grad_attn.reshape(tok_rows, head_count, DH)
        delta_sum = jnp.einsum(
            "tnd,tnd->nt", grad_heads, attn_heads, preferred_element_type=jnp.float32
        )
        grad_query = jnp.zeros((tok_rows, head_count, DH), jnp.float32)
        grad_key = grad_value = None
        for cycle_step in range(cycle_reach + 1):
            key_block, value_block, pair_mask = stored_blocks[cycle_step]
            scores = scores_of(query_heads, key_block)
            weights = jnp.where(pair_mask[None], jnp.exp(scores - log_total[..., None]), 0.0)
            rounded = weights.astype(jnp.bfloat16)
            value_part = jnp.einsum(
                "nts,tnd->snd", rounded, grad_heads, preferred_element_type=jnp.float32
            )
            grad_weights = jnp.einsum(
                "tnd,snd->nts", grad_heads, value_block, preferred_element_type=jnp.float32
            )
            grad_scores = (weights * (grad_weights - delta_sum[..., None])).astype(jnp.bfloat16)
            query_part = (
                jnp.einsum("nts,snd->tnd", grad_scores, key_block, preferred_element_type=jnp.float32)
                * score_scale
            )
            key_part = (
                jnp.einsum("nts,tnd->snd", grad_scores, query_heads, preferred_element_type=jnp.float32)
                * score_scale
            )
            grad_query = grad_query + query_part
            key_part = key_part.reshape(tok_rows, feature_width)
            value_part = value_part.reshape(tok_rows, feature_width)
            if cycle_step == 0:
                grad_key, grad_value = key_part, value_part
            else:
                sent = jnp.concatenate([key_part, value_part], axis=1).astype(jnp.bfloat16)
                back = shifted_by(sent, devices, -cycle_step).astype(jnp.float32)
                grad_key = grad_key + back[:, :feature_width]
                grad_value = grad_value + back[:, feature_width:]
        return (
            grad_query.reshape(tok_rows, feature_width).astype(jnp.bfloat16),
            grad_key.astype(jnp.bfloat16),
            grad_value.astype(jnp.bfloat16),
            grad_weight,
        )

    return shards


def solution(mesh):
    devices = mesh.shape["ctx"]
    fine = Mesh(mesh.devices.reshape(*CTX_SPLIT, 2, mesh.shape["fsdp"] // 2), CTX + FS)
    return jax.shard_map(
        make_shards(devices),
        mesh=fine,
        in_specs=(
            P(CTX, FS),
            P(CTX, FS),
            P(CTX, FS),
            P(CTX),
            P(FS + CTX, None),
            P(CTX, FS),
        ),
        out_specs=(P(CTX, FS), P(CTX, FS), P(CTX, FS), P(FS + CTX, None)),
        check_vma=False,
    )
```

time: 717 us -> 570 us (0.79)
  waiting for transfers between devices: 591 us -> 306 us
  local copies, waits for them, and re-layouts: 13 us -> 47.4 us
  starting transfers between devices: 51.4 us -> 84 us
  matrix products: 34.5 us -> 65.2 us
  other arithmetic: 6.71 us -> 32.5 us
  blocking collectives: 0 us -> 14.3 us
    ppermute x42 -> x24, waiting for transfers between devices: 230 us -> 110 us  [shifted_by(): return lax.ppermute(array, CTX, pairs)]
    all_gather x2 -> x3, waiting for transfers between devices: 145 us -> 46.9 us  [the longest x2 46.9 us: shards(): weight_rows = lax.all_gather(weight_rows, axis, axis=0, tiled=True)]
    reduce_scatter x1 -> x3, waiting for transfers between devices: 214 us -> 149 us  [shards(): lax.psum_scatter(partial_weight, axis, scatter_dimension=0, tiled=True)]
    ppermute x42 -> x24, starting transfers between devices: 51.3 us -> 83.1 us  [shifted_by(): return lax.ppermute(array, CTX, pairs)]
    reshape x1 -> x20, local copies, waits for them, and re-layouts: 0.17 us -> 24.2 us  [the longest x9 12 us: shards(): value_part = value_part.reshape(tok_rows, feature_width)]
    all_gather x0 -> x1, blocking collectives: none -> 14.3 us  [shards(): weight_rows = lax.all_gather(weight_rows, axis, axis=0, tiled=True)]
    concatenate x0 -> x9, other arithmetic: none -> 13.9 us  [the longest x8 13 us: shards(): sent = jnp.concatenate([key_part, value_part], axis=1).astype(jnp.bfloat16)]
    dot_general x9, matrix products: 2.99 us -> 15.9 us  [shards(): jnp.einsum('nts,tnd->snd', rounded, grad_heads, preferred_element_type=jn...]
  transfers between devices with their start and end apart: 45 -> 30, of which waited for: 41 -> 10; matrix products, arithmetic and copies ran while one was open for 6% -> 22% of each run, Pallas kernels for 0% -> 0%
where the time goes in v1:
time: 570 us; the launch traced here: 566 us
  waiting for transfers between devices  306 us (54%)
  starting transfers between devices  84 us (15%)
  matrix products  65.2 us (11%)
  local copies, waits for them, and re-layouts  47.4 us (8%)
  other arithmetic  32.5 us (6%)
  between operations  16.2 us (3%)
  blocking collectives  14.3 us (3%)
    reduce_scatter x3, waiting for transfers between devices, shards(): lax.psum_scatter(partial_weight, axis, scatter_dimension=0, tiled=True)  149 us
    ppermute x24, waiting for transfers between devices, shifted_by(): return lax.ppermute(array, CTX, pairs)  110 us
    ppermute x24, starting transfers between devices, shifted_by(): return lax.ppermute(array, CTX, pairs)  83.1 us
    all_gather x2, waiting for transfers between devices, shards(): weight_rows = lax.all_gather(weight_rows, axis, axis=0, tiled=True)  46.9 us
    dot_general x9, matrix products, shards(): jnp.einsum('nts,tnd->snd', rounded, grad_heads, preferred_element_type=jn...  15.9 us
    all_gather x1, blocking collectives, shards(): weight_rows = lax.all_gather(weight_rows, axis, axis=0, tiled=True)  14.3 us
    dot_general x9, matrix products, shards(): jnp.einsum('nts,tnd->snd', grad_scores, query_heads, preferred_element_ty...  13.6 us
    concatenate x8, other arithmetic, shards(): sent = jnp.concatenate([key_part, value_part], axis=1).astype(jnp.bfloat16)  13 us
  transfers between devices with their start and end apart: 30, of which 10 were waited for; matrix products, arithmetic and copies ran while one was open for 22% of the time, Pallas kernels for 0%

profile of v1, /device:TPU:8, one launch (start us, length us, event | category | flops | bytes accessed | tf_op | source)
XLA Modules:
  0.0 565.6 jit_solution(2665448239718029278)
XLA Ops:
  7.2 14.3 %all_gather.13 = bf16[32,4096]{1,0:T(8,128)(2,1)} all-gather(bf16[8,4096]{1,0:T(8,128)(2,1)} %param.10), channel_id=1, replica_groups=mesh['cy'=2,'cz'=8,'cx'=4,'fy'=2,'fc'=2] {'cx'}, dimensions={0}, use_global_device_ids=true | all-gather | bytes 327680 | tf_op jit(solution)/shard_map/all_gather | solution.py:39
  22.3 3.7 collective-permute-start.4
  26.0 3.8 collective-permute-start.6
  29.8 4.9 collective-permute-start.8
  34.7 5.9 %collective-permute-start.10 = (s32[256]{0:T(256)S(1)}, s32[256]{0:T(256)S(1)}, u32[]{:S(2)}, u32[]{:S(2)}) collective-permute-start(s32[256]{0:T(256)S(1)} %broadcast_add_fusion), channel_id=1, source_target_pairs={{0,24},{4,28},{8,32},{12,36},{16,40},{20,44},{24,48},{28,52},{32,5... | collective-permute-start | bytes 3080 | tf_op jit(solution)/shard_map/ppermute | solution.py:20
  40.6 4.6 collective-permute-start.12
  48.5 2.4 collective-permute-start.14
  50.9 4.1 collective-permute-start.2
  55.1 1.9 collective-permute-start
  57.0 1.9 collective-permute-start.15
  59.1 4.4 collective-permute-start.13
  63.5 1.9 collective-permute-start.11
  65.5 1.9 collective-permute-start.9
  67.4 2.5 collective-permute-start.7
  71.2 15.0 %collective-permute-done.15 = bf16[256,1024]{0,1:T(8,128)(2,1)S(1)} collective-permute-done((bf16[256,1024]{0,1:T(8,128)(2,1)}, bf16[256,1024]{0,1:T(8,128)(2,1)S(1)}, u32[]{:S(2)}, u32[]{:S(2)}) %collective-permute-start.15) | collective-permute-done | bytes 524320 | tf_op jit(solution)/shard_map/ppermute | solution.py:20
  87.1 5.3 collective-permute-start.5
  94.2 16.1 %collective-permute-done.13 = bf16[256,1024]{0,1:T(8,128)(2,1)S(1)} collective-permute-done((bf16[256,1024]{0,1:T(8,128)(2,1)}, bf16[256,1024]{0,1:T(8,128)(2,1)S(1)}, u32[]{:S(2)}, u32[]{:S(2)}) %collective-permute-start.13) | collective-permute-done | bytes 524320 | tf_op jit(solution)/shard_map/ppermute | solution.py:20
  110.3 3.1 collective-permute-start.3
  114.1 23.7 %collective-permute-done.11 = bf16[256,1024]{0,1:T(8,128)(2,1)S(1)} collective-permute-done((bf16[256,1024]{0,1:T(8,128)(2,1)}, bf16[256,1024]{0,1:T(8,128)(2,1)S(1)}, u32[]{:S(2)}, u32[]{:S(2)}) %collective-permute-start.11) | collective-permute-done | bytes 524320 | tf_op jit(solution)/shard_map/ppermute | solution.py:20
  140.5 16.7 %collective-permute-done.9 = bf16[256,1024]{0,1:T(8,128)(2,1)S(1)} collective-permute-done((bf16[256,1024]{0,1:T(8,128)(2,1)}, bf16[256,1024]{0,1:T(8,128)(2,1)S(1)}, u32[]{:S(2)}, u32[]{:S(2)}) %collective-permute-start.9) | collective-permute-done | bytes 524320 | tf_op jit(solution)/shard_map/ppermute | solution.py:20
  159.5 16.6 %collective-permute-done.3 = bf16[256,1024]{0,1:T(8,128)(2,1)S(1)} collective-permute-done((bf16[256,1024]{0,1:T(8,128)(2,1)}, bf16[256,1024]{0,1:T(8,128)(2,1)S(1)}, u32[]{:S(2)}, u32[]{:S(2)}) %collective-permute-start.3) | collective-permute-done | bytes 524320 | tf_op jit(solution)/shard_map/ppermute | solution.py:20
  176.9 21.3 %collective-permute-done.1 = bf16[256,1024]{0,1:T(8,128)(2,1)S(1)} collective-permute-done((bf16[256,1024]{0,1:T(8,128)(2,1)}, bf16[256,1024]{0,1:T(8,128)(2,1)S(1)}, u32[]{:S(2)}, u32[]{:S(2)}) %collective-permute-start.1) | collective-permute-done | bytes 524320 | tf_op jit(solution)/shard_map/ppermute | solution.py:20
  224.8 46.9 %all-gather.8.cloned.1.call-done = bf16[512,4096]{1,0:T(8,128)(2,1)} async-done(((bf16[256,4096]{1,0:T(8,128)(2,1)}), bf16[512,4096]{1,0:T(8,128)(2,1)}) %all-gather.8.cloned.1.call-update) | async-done | bytes 4194320 | tf_op jit(solution)/shard_map/all_gather | solution.py:39
  271.7 4.1 convolution_convert_fusion.8
  276.9 2.1 copy.286
  279.0 3.1 multiply_reduce_fusion
  283.4 3.9 copy.261
  304.4 2.3 convolution_convert_fusion
  308.5 2.1 fusion.70
  314.2 7.8 %collective-permute-start.23 = (bf16[256,1024]{1,0:T(8,128)(2,1)}, bf16[256,1024]{1,0:T(8,128)(2,1)}, u32[]{:S(2)}, u32[]{:S(2)}) collective-permute-start(bf16[256,1024]{1,0:T(8,128)(2,1)} %pad_maximum_fusion.8), channel_id=1, source_target_pairs={{32,0},{36,4},{40,8},{44,12},{48,16},{52,20},{56,24},{60,28},{64,3... | collective-permute-start | bytes 1572872 | tf_op jit(solution)/shard_map/ppermute | solution.py:20
  322.0 2.3 convolution_convert_fusion.1
  326.0 2.1 fusion.69
  331.8 5.1 collective-permute-start.22
  336.9 2.3 convolution_convert_fusion.2
  341.0 2.1 fusion.68
  346.7 4.5 collective-permute-start.21
  351.3 2.3 convolution_convert_fusion.3
  355.3 2.0 fusion.67
  361.1 3.2 collective-permute-start.20
  364.3 2.3 convolution_convert_fusion.4
  368.4 2.1 fusion.66
  374.1 2.4 collective-permute-start.19
  376.5 107.5 %reduce-scatter.4.cloned.1.call-done = f32[64,4096]{1,0:T(8,128)} async-done(((f32[512,4096]{1,0:T(8,128)}), f32[64,4096]{1,0:T(8,128)}) %reduce-scatter.4.cloned.1.call-update) | async-done | bytes 1048592 | tf_op jit(solution)/shard_map/reduce_scatter | solution.py:97
  484.4 2.3 convolution_convert_fusion.5
  501.8 1.9 collective-permute-start.17
  503.8 1.9 collective-permute-start.16
  506.2 32.1 %reduce-scatter.6.cloned.1.call-done = f32[16,4096]{1,0:T(8,128)} async-done(((f32[64,4096]{1,0:T(8,128)}), f32[16,4096]{1,0:T(8,128)}) %reduce-scatter.6.cloned.1.call-update) | async-done | bytes 262160 | tf_op jit(solution)/shard_map/reduce_scatter | solution.py:97
  548.9 9.8 %reduce-scatter.8.cloned.1.call-done = f32[8,4096]{1,0:T(8,128)} async-done(((f32[16,4096]{1,0:T(8,128)}), f32[8,4096]{1,0:T(8,128)}) %reduce-scatter.8.cloned.1.call-update) | async-done | bytes 131088 | tf_op jit(solution)/shard_map/reduce_scatter | solution.py:97
  (436 shorter events, 112.8 us)
Async XLA Ops:
  7.2 51.8 %copy-start.89 = (bf16[256,512]{1,0:T(8,128)(2,1)S(1)}, bf16[256,512]{1,0:T(8,128)(2,1)}, u32[]{:S(2)}) copy-start(bf16[256,512]{1,0:T(8,128)(2,1)} %param.6) | copy-start | bytes 786436
  7.2 201.6 %all-gather.6.cloned.1.call-start = ((), (), s32[]{:S(2)}) async-start(), calls=%async_computation.4 | async-start | bytes 2359296 | tf_op jit(solution)/shard_map/all_gather | solution.py:39
  21.6 203.3 %all-gather.4.cloned.1.call-start = ((), (), s32[]{:S(2)}) async-start(), calls=%async_computation.3 | async-start | bytes 2621440 | tf_op jit(solution)/shard_map/all_gather | solution.py:36
  22.3 26.2 %collective-permute-start.4 = (s32[256]{0:T(256)S(1)}, s32[256]{0:T(256)S(1)}, u32[]{:S(2)}, u32[]{:S(2)}) collective-permute-start(s32[256]{0:T(256)S(1)} %broadcast_add_fusion), channel_id=1, source_target_pairs={{0,12},{4,16},{8,20},{12,24},{16,28},{20,32},{24,36},{28,40},{32,4... | collective-permute-start | bytes 3080 | tf_op jit(solution)/shard_map/ppermute | solution.py:20
  26.0 24.9 %collective-permute-start.6 = (s32[256]{0:T(256)S(1)}, s32[256]{0:T(256)S(1)}, u32[]{:S(2)}, u32[]{:S(2)}) collective-permute-start(s32[256]{0:T(256)S(1)} %broadcast_add_fusion), channel_id=1, source_target_pairs={{0,16},{4,20},{8,24},{12,28},{16,32},{20,36},{24,40},{28,44},{32,4... | collective-permute-start | bytes 3080 | tf_op jit(solution)/shard_map/ppermute | solution.py:20
  29.8 25.2 %collective-permute-start.8 = (s32[256]{0:T(256)S(1)}, s32[256]{0:T(256)S(1)}, u32[]{:S(2)}, u32[]{:S(2)}) collective-permute-start(s32[256]{0:T(256)S(1)} %broadcast_add_fusion), channel_id=1, source_target_pairs={{0,20},{4,24},{8,28},{12,32},{16,36},{20,40},{24,44},{28,48},{32,5... | collective-permute-start | bytes 3080 | tf_op jit(solution)/shard_map/ppermute | solution.py:20
  34.7 22.3 %collective-permute-start.10 = (s32[256]{0:T(256)S(1)}, s32[256]{0:T(256)S(1)}, u32[]{:S(2)}, u32[]{:S(2)}) collective-permute-start(s32[256]{0:T(256)S(1)} %broadcast_add_fusion), channel_id=1, source_target_pairs={{0,24},{4,28},{8,32},{12,36},{16,40},{20,44},{24,48},{28,52},{32,5... | collective-permute-start | bytes 3080 | tf_op jit(solution)/shard_map/ppermute | solution.py:20
  40.6 18.5 %collective-permute-start.12 = (s32[256]{0:T(256)S(1)}, s32[256]{0:T(256)S(1)}, u32[]{:S(2)}, u32[]{:S(2)}) collective-permute-start(s32[256]{0:T(256)S(1)} %broadcast_add_fusion), channel_id=1, source_target_pairs={{0,28},{4,32},{8,36},{12,40},{16,44},{20,48},{24,52},{28,56},{32,6... | collective-permute-start | bytes 3080 | tf_op jit(solution)/shard_map/ppermute | solution.py:20
  45.3 226.5 %all-gather.8.cloned.1.call-start = ((), (), s32[]{:S(2)}) async-start(), calls=%async_computation.5 | async-start | bytes 6291456 | tf_op jit(solution)/shard_map/all_gather | solution.py:39
  46.4 24.8 %copy-start.23 = (bf16[256,512]{0,1:T(8,128)(2,1)}, bf16[256,512]{0,1:T(8,128)(2,1)S(1)}, u32[]{:S(2)}) copy-start(bf16[256,512]{0,1:T(8,128)(2,1)S(1)} %copy.331) | copy-start | bytes 786436
  48.5 15.0 %collective-permute-start.14 = (s32[256]{0:T(256)S(1)}, s32[256]{0:T(256)S(1)}, u32[]{:S(2)}, u32[]{:S(2)}) collective-permute-start(s32[256]{0:T(256)S(1)} %broadcast_add_fusion), channel_id=1, source_target_pairs={{0,32},{4,36},{8,40},{12,44},{16,48},{20,52},{24,56},{28,60},{32,6... | collective-permute-start | bytes 3080 | tf_op jit(solution)/shard_map/ppermute | solution.py:20
  50.9 14.5 %collective-permute-start.2 = (s32[256]{0:T(256)S(1)}, s32[256]{0:T(256)S(1)}, u32[]{:S(2)}, u32[]{:S(2)}) collective-permute-start(s32[256]{0:T(256)S(1)} %broadcast_add_fusion), channel_id=1, source_target_pairs={{0,8},{4,12},{8,16},{12,20},{16,24},{20,28},{24,32},{28,36},{32,40... | collective-permute-start | bytes 3080 | tf_op jit(solution)/shard_map/ppermute | solution.py:20
  55.1 12.3 %collective-permute-start = (s32[256]{0:T(256)S(1)}, s32[256]{0:T(256)S(1)}, u32[]{:S(2)}, u32[]{:S(2)}) collective-permute-start(s32[256]{0:T(256)S(1)} %broadcast_add_fusion), channel_id=1, source_target_pairs={{0,4},{4,8},{8,12},{12,16},{16,20},{20,24},{24,28},{28,32},{32,36}... | collective-permute-start | bytes 3080 | tf_op jit(solution)/shard_map/ppermute | solution.py:20
  57.0 29.3 %collective-permute-start.15 = (bf16[256,1024]{0,1:T(8,128)(2,1)}, bf16[256,1024]{0,1:T(8,128)(2,1)S(1)}, u32[]{:S(2)}, u32[]{:S(2)}) collective-permute-start(bf16[256,1024]{0,1:T(8,128)(2,1)} %pad_maximum_fusion), channel_id=1, source_target_pairs={{0,32},{4,36},{8,40},{12,44},{16,48},{20,52},{24,56},{28,60},{32,6... | collective-permute-start | bytes 1572872 | tf_op jit(solution)/shard_map/ppermute | solution.py:20
  59.1 51.1 %collective-permute-start.13 = (bf16[256,1024]{0,1:T(8,128)(2,1)}, bf16[256,1024]{0,1:T(8,128)(2,1)S(1)}, u32[]{:S(2)}, u32[]{:S(2)}) collective-permute-start(bf16[256,1024]{0,1:T(8,128)(2,1)} %pad_maximum_fusion), channel_id=1, source_target_pairs={{0,28},{4,32},{8,36},{12,40},{16,44},{20,48},{24,52},{28,56},{32,6... | collective-permute-start | bytes 1572872 | tf_op jit(solution)/shard_map/ppermute | solution.py:20
  63.5 74.3 %collective-permute-start.11 = (bf16[256,1024]{0,1:T(8,128)(2,1)}, bf16[256,1024]{0,1:T(8,128)(2,1)S(1)}, u32[]{:S(2)}, u32[]{:S(2)}) collective-permute-start(bf16[256,1024]{0,1:T(8,128)(2,1)} %pad_maximum_fusion), channel_id=1, source_target_pairs={{0,24},{4,28},{8,32},{12,36},{16,40},{20,44},{24,48},{28,52},{32,5... | collective-permute-start | bytes 1572872 | tf_op jit(solution)/shard_map/ppermute | solution.py:20
  65.5 91.7 %collective-permute-start.9 = (bf16[256,1024]{0,1:T(8,128)(2,1)}, bf16[256,1024]{0,1:T(8,128)(2,1)S(1)}, u32[]{:S(2)}, u32[]{:S(2)}) collective-permute-start(bf16[256,1024]{0,1:T(8,128)(2,1)} %pad_maximum_fusion), channel_id=1, source_target_pairs={{0,20},{4,24},{8,28},{12,32},{16,36},{20,40},{24,44},{28,48},{32,5... | collective-permute-start | bytes 1572872 | tf_op jit(solution)/shard_map/ppermute | solution.py:20
  67.4 90.5 %collective-permute-start.7 = (bf16[256,1024]{0,1:T(8,128)(2,1)}, bf16[256,1024]{0,1:T(8,128)(2,1)S(1)}, u32[]{:S(2)}, u32[]{:S(2)}) collective-permute-start(bf16[256,1024]{0,1:T(8,128)(2,1)} %pad_maximum_fusion), channel_id=1, source_target_pairs={{0,16},{4,20},{8,24},{12,28},{16,32},{20,36},{24,40},{28,44},{32,4... | collective-permute-start | bytes 1572872 | tf_op jit(solution)/shard_map/ppermute | solution.py:20
  70.8 69.7 %copy-start.69 = (pred[256,256]{0,1:T(8,128)(4,1)}, pred[256,256]{0,1:T(8,128)(4,1)S(1)}, u32[]{:S(2)}) copy-start(pred[256,256]{0,1:T(8,128)(4,1)S(1)} %get-tuple-element.51) | copy-start | bytes 196612
  70.8 128.2 %copy-start.65 = (pred[256,256]{0,1:T(8,128)(4,1)}, pred[256,256]{0,1:T(8,128)(4,1)S(1)}, u32[]{:S(2)}) copy-start(pred[256,256]{0,1:T(8,128)(4,1)S(1)} %get-tuple-element.57) | copy-start | bytes 196612
  70.8 129.6 %copy-start.61 = (pred[256,256]{0,1:T(8,128)(4,1)}, pred[256,256]{0,1:T(8,128)(4,1)S(1)}, u32[]{:S(2)}) copy-start(pred[256,256]{0,1:T(8,128)(4,1)S(1)} %get-tuple-element.56) | copy-start | bytes 196612
  70.8 130.9 %copy-start.57 = (pred[256,256]{0,1:T(8,128)(4,1)}, pred[256,256]{0,1:T(8,128)(4,1)S(1)}, u32[]{:S(2)}) copy-start(pred[256,256]{0,1:T(8,128)(4,1)S(1)} %get-tuple-element.55) | copy-start | bytes 196612
  70.8 132.3 %copy-start.53 = (pred[256,256]{0,1:T(8,128)(4,1)}, pred[256,256]{0,1:T(8,128)(4,1)S(1)}, u32[]{:S(2)}) copy-start(pred[256,256]{0,1:T(8,128)(4,1)S(1)} %get-tuple-element.54) | copy-start | bytes 196612
  70.8 133.6 %copy-start.49 = (pred[256,256]{0,1:T(8,128)(4,1)}, pred[256,256]{0,1:T(8,128)(4,1)S(1)}, u32[]{:S(2)}) copy-start(pred[256,256]{0,1:T(8,128)(4,1)S(1)} %get-tuple-element.53) | copy-start | bytes 196612
  70.8 135.0 %copy-start.45 = (pred[256,256]{0,1:T(8,128)(4,1)}, pred[256,256]{0,1:T(8,128)(4,1)S(1)}, u32[]{:S(2)}) copy-start(pred[256,256]{0,1:T(8,128)(4,1)S(1)} %get-tuple-element.52) | copy-start | bytes 196612
  87.1 71.6 %collective-permute-start.5 = (bf16[256,1024]{0,1:T(8,128)(2,1)}, bf16[256,1024]{0,1:T(8,128)(2,1)S(1)}, u32[]{:S(2)}, u32[]{:S(2)}) collective-permute-start(bf16[256,1024]{0,1:T(8,128)(2,1)} %pad_maximum_fusion), channel_id=1, source_target_pairs={{0,12},{4,16},{8,20},{12,24},{16,28},{20,32},{24,36},{28,40},{32,4... | collective-permute-start | bytes 1572872 | tf_op jit(solution)/shard_map/ppermute | solution.py:20
  94.2 104.8 %copy-start.43 = (bf16[256,512]{0,1:T(8,128)(2,1)}, bf16[256,512]{0,1:T(8,128)(2,1)S(1)}, u32[]{:S(2)}) copy-start(bf16[256,512]{0,1:T(8,128)(2,1)S(1)} %get-tuple-element.46) | copy-start | bytes 786436
  110.3 65.9 %collective-permute-start.3 = (bf16[256,1024]{0,1:T(8,128)(2,1)}, bf16[256,1024]{0,1:T(8,128)(2,1)S(1)}, u32[]{:S(2)}, u32[]{:S(2)}) collective-permute-start(bf16[256,1024]{0,1:T(8,128)(2,1)} %pad_maximum_fusion), channel_id=1, source_target_pairs={{0,8},{4,12},{8,16},{12,20},{16,24},{20,28},{24,32},{28,36},{32,40... | collective-permute-start | bytes 1572872 | tf_op jit(solution)/shard_map/ppermute | solution.py:20
  114.1 86.3 %copy-start.25 = (bf16[256,512]{0,1:T(8,128)(2,1)}, bf16[256,512]{0,1:T(8,128)(2,1)S(1)}, u32[]{:S(2)}) copy-start(bf16[256,512]{0,1:T(8,128)(2,1)S(1)} %get-tuple-element.45) | copy-start | bytes 786436
  137.8 60.5 %collective-permute-start.1 = (bf16[256,1024]{0,1:T(8,128)(2,1)}, bf16[256,1024]{0,1:T(8,128)(2,1)S(1)}, u32[]{:S(2)}, u32[]{:S(2)}) collective-permute-start(bf16[256,1024]{0,1:T(8,128)(2,1)} %pad_maximum_fusion), channel_id=1, source_target_pairs={{0,4},{4,8},{8,12},{12,16},{16,20},{20,24},{24,28},{28,32},{32,36}... | collective-permute-start | bytes 1572872 | tf_op jit(solution)/shard_map/ppermute | solution.py:20
  140.5 61.3 %copy-start.27 = (bf16[256,512]{0,1:T(8,128)(2,1)}, bf16[256,512]{0,1:T(8,128)(2,1)S(1)}, u32[]{:S(2)}) copy-start(bf16[256,512]{0,1:T(8,128)(2,1)S(1)} %get-tuple-element.43) | copy-start | bytes 786436
  157.9 45.2 %copy-start.29 = (bf16[256,512]{0,1:T(8,128)(2,1)}, bf16[256,512]{0,1:T(8,128)(2,1)S(1)}, u32[]{:S(2)}) copy-start(bf16[256,512]{0,1:T(8,128)(2,1)S(1)} %get-tuple-element.41) | copy-start | bytes 786436
  158.7 45.7 %copy-start.31 = (bf16[256,512]{0,1:T(8,128)(2,1)}, bf16[256,512]{0,1:T(8,128)(2,1)S(1)}, u32[]{:S(2)}) copy-start(bf16[256,512]{0,1:T(8,128)(2,1)S(1)} %get-tuple-element.39) | copy-start | bytes 786436
  159.5 46.3 %copy-start.33 = (bf16[256,512]{0,1:T(8,128)(2,1)}, bf16[256,512]{0,1:T(8,128)(2,1)S(1)}, u32[]{:S(2)}) copy-start(bf16[256,512]{0,1:T(8,128)(2,1)S(1)} %get-tuple-element.37) | copy-start | bytes 786436
  176.9 30.3 %copy-start.35 = (bf16[256,512]{0,1:T(8,128)(2,1)}, bf16[256,512]{0,1:T(8,128)(2,1)S(1)}, u32[]{:S(2)}) copy-start(bf16[256,512]{0,1:T(8,128)(2,1)S(1)} %get-tuple-element.35) | copy-start | bytes 786436
  208.8 275.3 %reduce-scatter.4.cloned.1.call-start = ((), (), s32[]{:S(2)}) async-start(), calls=%async_computation.6 | async-start | bytes 9437184 | tf_op jit(solution)/shard_map/reduce_scatter | solution.py:97
  287.5 250.8 %reduce-scatter.6.cloned.1.call-start = ((), (), s32[]{:S(2)}) async-start(), calls=%async_computation.7 | async-start | bytes 1310720 | tf_op jit(solution)/shard_map/reduce_scatter | solution.py:97
  314.2 185.7 %collective-permute-start.23 = (bf16[256,1024]{1,0:T(8,128)(2,1)}, bf16[256,1024]{1,0:T(8,128)(2,1)}, u32[]{:S(2)}, u32[]{:S(2)}) collective-permute-start(bf16[256,1024]{1,0:T(8,128)(2,1)} %pad_maximum_fusion.8), channel_id=1, source_target_pairs={{32,0},{36,4},{40,8},{44,12},{48,16},{52,20},{56,24},{60,28},{64,3... | collective-permute-start | bytes 1572872 | tf_op jit(solution)/shard_map/ppermute | solution.py:20
  331.8 170.0 %collective-permute-start.22 = (bf16[256,1024]{1,0:T(8,128)(2,1)}, bf16[256,1024]{1,0:T(8,128)(2,1)}, u32[]{:S(2)}, u32[]{:S(2)}) collective-permute-start(bf16[256,1024]{1,0:T(8,128)(2,1)} %pad_maximum_fusion.7), channel_id=1, source_target_pairs={{28,0},{32,4},{36,8},{40,12},{44,16},{48,20},{52,24},{56,28},{60,3... | collective-permute-start | bytes 1572872 | tf_op jit(solution)/shard_map/ppermute | solution.py:20
  346.7 157.1 %collective-permute-start.21 = (bf16[256,1024]{1,0:T(8,128)(2,1)}, bf16[256,1024]{1,0:T(8,128)(2,1)}, u32[]{:S(2)}, u32[]{:S(2)}) collective-permute-start(bf16[256,1024]{1,0:T(8,128)(2,1)} %pad_maximum_fusion.6), channel_id=1, source_target_pairs={{24,0},{28,4},{32,8},{36,12},{40,16},{44,20},{48,24},{52,28},{56,3... | collective-permute-start | bytes 1572872 | tf_op jit(solution)/shard_map/ppermute | solution.py:20
  361.1 181.3 %collective-permute-start.20 = (bf16[256,1024]{1,0:T(8,128)(2,1)}, bf16[256,1024]{1,0:T(8,128)(2,1)}, u32[]{:S(2)}, u32[]{:S(2)}) collective-permute-start(bf16[256,1024]{1,0:T(8,128)(2,1)} %pad_maximum_fusion.5), channel_id=1, source_target_pairs={{20,0},{24,4},{28,8},{32,12},{36,16},{40,20},{44,24},{48,28},{52,3... | collective-permute-start | bytes 1572872 | tf_op jit(solution)/shard_map/ppermute | solution.py:20
  366.6 117.8 %copy-start.48 = (pred[256,256]{0,1:T(8,128)(4,1)S(1)}, pred[256,256]{0,1:T(8,128)(4,1)}, u32[]{:S(2)}) copy-start(pred[256,256]{0,1:T(8,128)(4,1)} %copy-done.45) | copy-start | bytes 196612
  374.1 169.4 %collective-permute-start.19 = (bf16[256,1024]{1,0:T(8,128)(2,1)}, bf16[256,1024]{1,0:T(8,128)(2,1)}, u32[]{:S(2)}, u32[]{:S(2)}) collective-permute-start(bf16[256,1024]{1,0:T(8,128)(2,1)} %pad_maximum_fusion.4), channel_id=1, source_target_pairs={{16,0},{20,4},{24,8},{28,12},{32,16},{36,20},{40,24},{44,28},{48,3... | collective-permute-start | bytes 1572872 | tf_op jit(solution)/shard_map/ppermute | solution.py:20
  484.1 74.6 %reduce-scatter.8.cloned.1.call-start = ((), (), s32[]{:S(2)}) async-start(), calls=%async_computation.8 | async-start | bytes 393216 | tf_op jit(solution)/shard_map/reduce_scatter | solution.py:97
  499.0 39.4 %copy-start.22 = (bf16[4,256,256]{1,2,0:T(8,128)(2,1)S(1)}, bf16[4,256,256]{1,2,0:T(8,128)(2,1)}, u32[]{:S(2)}) copy-start(bf16[4,256,256]{1,2,0:T(8,128)(2,1)} %copy-done.21) | copy-start | bytes 1572868
  499.9 44.8 %collective-permute-start.18 = (bf16[256,1024]{1,0:T(8,128)(2,1)}, bf16[256,1024]{1,0:T(8,128)(2,1)S(1)}, u32[]{:S(2)}, u32[]{:S(2)}) collective-permute-start(bf16[256,1024]{1,0:T(8,128)(2,1)} %pad_maximum_fusion.3), channel_id=1, source_target_pairs={{12,0},{16,4},{20,8},{24,12},{28,16},{32,20},{36,24},{40,28},{44,3... | collective-permute-start | bytes 1572872 | tf_op jit(solution)/shard_map/ppermute | solution.py:20
  501.8 43.0 %collective-permute-start.17 = (bf16[256,1024]{1,0:T(8,128)(2,1)}, bf16[256,1024]{1,0:T(8,128)(2,1)}, u32[]{:S(2)}, u32[]{:S(2)}) collective-permute-start(bf16[256,1024]{1,0:T(8,128)(2,1)} %pad_maximum_fusion.2), channel_id=1, source_target_pairs={{8,0},{12,4},{16,8},{20,12},{24,16},{28,20},{32,24},{36,28},{40,32... | collective-permute-start | bytes 1572872 | tf_op jit(solution)/shard_map/ppermute | solution.py:20
  503.8 42.3 %collective-permute-start.16 = (bf16[256,1024]{1,0:T(8,128)(2,1)}, bf16[256,1024]{1,0:T(8,128)(2,1)}, u32[]{:S(2)}, u32[]{:S(2)}) collective-permute-start(bf16[256,1024]{1,0:T(8,128)(2,1)} %pad_maximum_fusion.1), channel_id=1, source_target_pairs={{4,0},{8,4},{12,8},{16,12},{20,16},{24,20},{28,24},{32,28},{36,32}... | collective-permute-start | bytes 1572872 | tf_op jit(solution)/shard_map/ppermute | solution.py:20
  (126 other events, 360.7 us)
Sparse Core Ops, SparseCore 0:
  21.7 52.4 all-gather.5
  76.0 76.7 all-gather.3
  208.9 62.7 all-gather.7
  287.6 196.4 reduce-scatter.3
  486.5 51.8 reduce-scatter.5
  541.3 17.4 reduce-scatter.7

commit v2 on v1

--- a/solution.py
+++ b/solution.py
@@ -20,6 +20,20 @@
     return lax.ppermute(array, CTX, pairs)
 
 
+def gathered_rows(rows, index, devices):
+    bits = [devices >> k for k in (2, 3, 5, 1, 4, 6) if devices >> k >= 1]
+    block = rows
+    for bit in bits:
+        other = lax.ppermute(block, CTX, [(i, i ^ bit) for i in range(devices)])
+        low = (index & bit) == 0
+        block = jnp.where(low, jnp.concatenate([block, other]), jnp.concatenate([other, block]))
+    order = sorted(range(len(bits)), key=lambda k: -bits[k])
+    shape = [2] * len(bits) + list(rows.shape)
+    block = block.reshape(shape)
+    block = block.transpose([len(bits) - 1 - k for k in order] + [len(bits), len(bits) + 1])
+    return block.reshape(devices * rows.shape[0], rows.shape[1])
+
+
 def make_shards(devices):
     def shards(query, key, value, doc_ids, out_weight, grad_out):
         tok_rows = query.shape[0]
@@ -34,15 +48,17 @@
         query_heads = query.reshape(tok_rows, head_count, DH)
 
         grad_full = lax.all_gather(grad_out, FS, axis=1, tiled=True)
-        weight_rows = out_weight
-        for axis in ("cx", "cz", "cy"):
-            weight_rows = lax.all_gather(weight_rows, axis, axis=0, tiled=True)
+        weight_rows = gathered_rows(out_weight, cycle_index, devices)
 
         key_value = jnp.concatenate([key, value], axis=1)
+        doc_row = jnp.zeros((1, 2 * feature_width), jnp.bfloat16)
+        doc_row = doc_row.at[0, :tok_rows].set(own_docs.astype(jnp.bfloat16))
+        key_value = jnp.concatenate([key_value, doc_row], axis=0)
         blocks = [(key, value, own_docs)]
         for cycle_step in range(1, cycle_reach + 1):
             got = shifted_by(key_value, devices, cycle_step)
-            got_docs = shifted_by(own_docs, devices, cycle_step)
+            got_docs = got[tok_rows, :tok_rows].astype(jnp.int32)
+            got = got[:tok_rows]
             blocks.append((got[:, :feature_width], got[:, feature_width:], got_docs))
 
         def scores_of(query_block, key_block):

time: 570 us -> 587 us (1.030)
  the two profiles are of different devices: /device:TPU:8 before, /device:TPU:1 now
where the time goes in v2:
time: 587 us; the launch traced here: 576 us
  waiting for transfers between devices  284 us (48%)
  starting transfers between devices  110 us (19%)
  matrix products  58.9 us (10%)
  local copies, waits for them, and re-layouts  57.7 us (10%)
  other arithmetic  49.3 us (8%)
  between operations  16.1 us (3%)
    reduce_scatter x3, waiting for transfers between devices, shards(): lax.psum_scatter(partial_weight, axis, scatter_dimension=0, tiled=True)  168 us
    ppermute x6, waiting for transfers between devices, gathered_rows(): other = lax.ppermute(block, CTX, [(i, i ^ bit) for i in range(devices)])  100 us
    ppermute x6, starting transfers between devices, gathered_rows(): other = lax.ppermute(block, CTX, [(i, i ^ bit) for i in range(devices)])  55.4 us
    ppermute x16, starting transfers between devices, shifted_by(): return lax.ppermute(array, CTX, pairs)  54.2 us
    dot_general x9, matrix products, shards(): jnp.einsum('nts,tnd->snd', rounded, grad_heads, preferred_element_type=jn...  16.2 us
    slice x16, local copies, waits for them, and re-layouts, shards(): blocks.append((got[:, :feature_width], got[:, feature_width:], got_docs))  16.1 us
    ppermute x16, waiting for transfers between devices, shifted_by(): return lax.ppermute(array, CTX, pairs)  15.9 us
    dot_general x9, matrix products, shards(): jnp.einsum('nts,tnd->snd', grad_scores, query_heads, preferred_element_ty...  15.3 us
  transfers between devices with their start and end apart: 26, of which 10 were waited for; matrix products, arithmetic and copies ran while one was open for 25% of the time, Pallas kernels for 0%

profile of v2, /device:TPU:1, one launch (start us, length us, event | category | flops | bytes accessed | tf_op | source)
XLA Modules:
  0.0 575.9 jit_solution(11757068906188507591)
XLA Ops:
  9.2 1.9 fusion.100
  11.2 5.7 collective-permute-start.7
  16.9 5.2 collective-permute-start.2
  22.1 3.6 collective-permute-start.3
  25.7 4.6 collective-permute-start.5
  32.0 37.8 %collective-permute-done.8 = bf16[8,4096]{1,0:T(8,128)(2,1)S(1)} collective-permute-done((bf16[8,4096]{1,0:T(8,128)(2,1)}, bf16[8,4096]{1,0:T(8,128)(2,1)S(1)}, u32[]{:S(2)}, u32[]{:S(2)}) %collective-permute-start.8) | collective-permute-done | bytes 65568 | tf_op jit(solution)/shard_map/ppermute | solution.py:27
  70.8 3.5 collective-permute-start.9
  74.8 2.3 collective-permute-done.9
  77.2 26.1 %collective-permute-start.10 = (bf16[32,4096]{1,0:T(8,128)(2,1)S(1)}, bf16[32,4096]{1,0:T(8,128)(2,1)}, u32[]{:S(2)}, u32[]{:S(2)}) collective-permute-start(bf16[32,4096]{1,0:T(8,128)(2,1)S(1)} %maximum_select_fusion.4), channel_id=1, source_target_pairs={{0,8},{4,12},{8,0},{12,4},{16,24},{20,28},{24,16},{28,20},{32,40},... | collective-permute-start | bytes 786440 | tf_op jit(solution)/shard_map/ppermute | solution.py:27
  106.2 2.4 collective-permute-done.10
  109.9 2.0 maximum_select_fusion.3
  113.2 6.7 %collective-permute-done.6 = bf16[257,1024]{1,0:T(8,128)(2,1)S(1)} collective-permute-done((bf16[257,1024]{1,0:T(8,128)(2,1)}, bf16[257,1024]{1,0:T(8,128)(2,1)S(1)}, u32[]{:S(2)}, u32[]{:S(2)}) %collective-permute-start.6) | collective-permute-done | bytes 526368 | tf_op jit(solution)/shard_map/ppermute | solution.py:20
  120.0 16.6 %collective-permute-start.1 = (bf16[257,1024]{1,0:T(8,128)(2,1)}, bf16[257,1024]{1,0:T(8,128)(2,1)}, u32[]{:S(2)}, u32[]{:S(2)}) collective-permute-start(bf16[257,1024]{1,0:T(8,128)(2,1)} %fusion.100), channel_id=1, source_target_pairs={{0,8},{4,12},{8,16},{12,20},{16,24},{20,28},{24,32},{28,36},{32,40... | collective-permute-start | bytes 1579016 | tf_op jit(solution)/shard_map/ppermute | solution.py:20
  136.6 5.2 collective-permute-start
  141.9 8.5 %collective-permute-start.11 = (bf16[64,4096]{1,0:T(8,128)(2,1)}, bf16[64,4096]{1,0:T(8,128)(2,1)}, u32[]{:S(2)}, u32[]{:S(2)}) collective-permute-start(bf16[64,4096]{1,0:T(8,128)(2,1)} %maximum_select_fusion.3), channel_id=1, source_target_pairs={{0,128},{4,132},{8,136},{12,140},{16,144},{20,148},{24,152},{28,15... | collective-permute-start | bytes 1572872 | tf_op jit(solution)/shard_map/ppermute | solution.py:27
  150.5 1.9 fusion.240
  155.9 1.9 fusion.238
  157.9 9.1 %collective-permute-done = bf16[257,1024]{1,0:T(8,128)(2,1)} collective-permute-done((bf16[257,1024]{1,0:T(8,128)(2,1)}, bf16[257,1024]{1,0:T(8,128)(2,1)}, u32[]{:S(2)}, u32[]{:S(2)}) %collective-permute-start) | collective-permute-done | bytes 526368 | tf_op jit(solution)/shard_map/ppermute | solution.py:20
  167.0 1.9 fusion.237
  191.9 16.2 %collective-permute-start.12 = (bf16[128,4096]{1,0:T(8,128)(2,1)S(1)}, bf16[128,4096]{1,0:T(8,128)(2,1)S(1)}, u32[]{:S(2)}, u32[]{:S(2)}) collective-permute-start(bf16[128,4096]{1,0:T(8,128)(2,1)S(1)} %maximum_select_fusion.2), channel_id=1, source_target_pairs={{0,16},{4,20},{8,24},{12,28},{16,0},{20,4},{24,8},{28,12},{32,48},... | collective-permute-start | bytes 3145736 | tf_op jit(solution)/shard_map/ppermute | solution.py:27
  210.1 21.0 %collective-permute-done.12 = bf16[128,4096]{1,0:T(8,128)(2,1)S(1)} collective-permute-done((bf16[128,4096]{1,0:T(8,128)(2,1)S(1)}, bf16[128,4096]{1,0:T(8,128)(2,1)S(1)}, u32[]{:S(2)}, u32[]{:S(2)}) %collective-permute-start.12) | collective-permute-done | bytes 1048608 | tf_op jit(solution)/shard_map/ppermute | solution.py:27
  241.0 36.8 %collective-permute-done.13 = bf16[256,4096]{1,0:T(8,128)(2,1)S(1)} collective-permute-done((bf16[256,4096]{1,0:T(8,128)(2,1)S(1)}, bf16[256,4096]{1,0:T(8,128)(2,1)S(1)}, u32[]{:S(2)}, u32[]{:S(2)}) %collective-permute-start.13) | collective-permute-done | bytes 2097184 | tf_op jit(solution)/shard_map/ppermute | solution.py:27
  277.9 2.2 maximum_select_fusion
  280.0 2.3 copy.389
  282.5 4.3 convolution_convert_fusion.8
  289.8 3.9 copy.490
  310.4 2.6 convolution_convert_fusion
  314.8 2.0 fusion.69
  318.6 1.9 pad_maximum_fusion.7
  322.0 2.3 convolution_convert_fusion.1
  326.0 2.1 fusion.68
  329.9 1.9 pad_maximum_fusion.6
  333.2 2.3 convolution_convert_fusion.2
  337.3 2.0 fusion.67
  341.1 1.9 pad_maximum_fusion.5
  344.5 2.3 convolution_convert_fusion.3
  348.6 2.1 fusion.66
  352.4 1.9 pad_maximum_fusion.4
  355.6 2.3 convolution_convert_fusion.4
  357.9 1.8 copy.467
  359.7 2.1 fusion.65
  363.6 1.9 pad_maximum_fusion.3
  366.8 109.8 %reduce-scatter.4.cloned.1.call-done = f32[64,4096]{1,0:T(8,128)} async-done(((f32[512,4096]{1,0:T(8,128)}), f32[64,4096]{1,0:T(8,128)}) %reduce-scatter.4.cloned.1.call-update) | async-done | bytes 1048592 | tf_op jit(solution)/shard_map/reduce_scatter | solution.py:113
  476.8 2.3 convolution_convert_fusion.5
  488.2 2.0 fusion.62
  491.4 1.9 pad_maximum_fusion.2
  499.5 52.6 %reduce-scatter.6.cloned.1.call-done = f32[16,4096]{1,0:T(8,128)} async-done(((f32[64,4096]{1,0:T(8,128)}), f32[16,4096]{1,0:T(8,128)}) %reduce-scatter.6.cloned.1.call-update) | async-done | bytes 262160 | tf_op jit(solution)/shard_map/reduce_scatter | solution.py:113
  563.8 5.1 reduce-scatter.8.cloned.1.call-done
  (395 shorter events, 119.3 us)
Async XLA Ops:
  7.2 96.9 %copy-start.55 = (bf16[256,512]{1,0:T(8,128)(2,1)S(1)}, bf16[256,512]{1,0:T(8,128)(2,1)}, u32[]{:S(2)}) copy-start(bf16[256,512]{1,0:T(8,128)(2,1)} %param.10) | copy-start | bytes 786436
  7.2 96.7 %copy-start.54 = (bf16[256,512]{1,0:T(8,128)(2,1)S(1)}, bf16[256,512]{1,0:T(8,128)(2,1)}, u32[]{:S(2)}) copy-start(bf16[256,512]{1,0:T(8,128)(2,1)} %param.9) | copy-start | bytes 786436
  7.2 97.7 %copy-start.88 = (bf16[256,512]{1,0:T(8,128)(2,1)S(1)}, bf16[256,512]{1,0:T(8,128)(2,1)}, u32[]{:S(2)}) copy-start(bf16[256,512]{1,0:T(8,128)(2,1)} %param.8) | copy-start | bytes 786436
  7.2 275.1 %all-gather.2.cloned.1.call-start = ((), (), s32[]{:S(2)}) async-start(), calls=%async_computation.3 | async-start | bytes 2621440 | tf_op jit(solution)/shard_map/all_gather | solution.py:50
  11.2 100.7 %collective-permute-start.7 = (bf16[257,1024]{1,0:T(8,128)(2,1)}, bf16[257,1024]{1,0:T(8,128)(2,1)S(1)}, u32[]{:S(2)}, u32[]{:S(2)}) collective-permute-start(bf16[257,1024]{1,0:T(8,128)(2,1)} %fusion.100), channel_id=1, source_target_pairs={{0,32},{4,36},{8,40},{12,44},{16,48},{20,52},{24,56},{28,60},{32,6... | collective-permute-start | bytes 1579016 | tf_op jit(solution)/shard_map/ppermute | solution.py:20
  16.9 137.1 %collective-permute-start.2 = (bf16[257,1024]{1,0:T(8,128)(2,1)}, bf16[257,1024]{1,0:T(8,128)(2,1)}, u32[]{:S(2)}, u32[]{:S(2)}) collective-permute-start(bf16[257,1024]{1,0:T(8,128)(2,1)} %fusion.100), channel_id=1, source_target_pairs={{0,12},{4,16},{8,20},{12,24},{16,28},{20,32},{24,36},{28,40},{32,4... | collective-permute-start | bytes 1579016 | tf_op jit(solution)/shard_map/ppermute | solution.py:20
  22.1 128.4 %collective-permute-start.3 = (bf16[257,1024]{1,0:T(8,128)(2,1)}, bf16[257,1024]{1,0:T(8,128)(2,1)}, u32[]{:S(2)}, u32[]{:S(2)}) collective-permute-start(bf16[257,1024]{1,0:T(8,128)(2,1)} %fusion.100), channel_id=1, source_target_pairs={{0,16},{4,20},{8,24},{12,28},{16,32},{20,36},{24,40},{28,44},{32,4... | collective-permute-start | bytes 1579016 | tf_op jit(solution)/shard_map/ppermute | solution.py:20
  25.7 110.9 %collective-permute-start.5 = (bf16[257,1024]{1,0:T(8,128)(2,1)}, bf16[257,1024]{1,0:T(8,128)(2,1)S(1)}, u32[]{:S(2)}, u32[]{:S(2)}) collective-permute-start(bf16[257,1024]{1,0:T(8,128)(2,1)} %fusion.100), channel_id=1, source_target_pairs={{0,24},{4,28},{8,32},{12,36},{16,40},{20,44},{24,48},{28,52},{32,5... | collective-permute-start | bytes 1579016 | tf_op jit(solution)/shard_map/ppermute | solution.py:20
  30.3 39.5 %collective-permute-start.8 = (bf16[8,4096]{1,0:T(8,128)(2,1)}, bf16[8,4096]{1,0:T(8,128)(2,1)S(1)}, u32[]{:S(2)}, u32[]{:S(2)}) collective-permute-start(bf16[8,4096]{1,0:T(8,128)(2,1)} %param.12), channel_id=1, source_target_pairs={{0,64},{4,68},{8,72},{12,76},{16,80},{20,84},{24,88},{28,92},{32,9... | collective-permute-start | bytes 196616 | tf_op jit(solution)/shard_map/ppermute | solution.py:27
  31.3 445.2 %reduce-scatter.4.cloned.1.call-start = ((), (), s32[]{:S(2)}) async-start(), calls=%async_computation.4 | async-start | bytes 9437184 | tf_op jit(solution)/shard_map/reduce_scatter | solution.py:113
  70.8 6.4 %collective-permute-start.9 = (bf16[16,4096]{1,0:T(8,128)(2,1)S(1)}, bf16[16,4096]{1,0:T(8,128)(2,1)S(1)}, u32[]{:S(2)}, u32[]{:S(2)}) collective-permute-start(bf16[16,4096]{1,0:T(8,128)(2,1)S(1)} %maximum_select_fusion.5), channel_id=1, source_target_pairs={{0,32},{4,36},{8,40},{12,44},{16,48},{20,52},{24,56},{28,60},{32,0... | collective-permute-start | bytes 393224 | tf_op jit(solution)/shard_map/ppermute | solution.py:27
  77.2 31.4 %collective-permute-start.10 = (bf16[32,4096]{1,0:T(8,128)(2,1)S(1)}, bf16[32,4096]{1,0:T(8,128)(2,1)}, u32[]{:S(2)}, u32[]{:S(2)}) collective-permute-start(bf16[32,4096]{1,0:T(8,128)(2,1)S(1)} %maximum_select_fusion.4), channel_id=1, source_target_pairs={{0,8},{4,12},{8,0},{12,4},{16,24},{20,28},{24,16},{28,20},{32,40},... | collective-permute-start | bytes 786440 | tf_op jit(solution)/shard_map/ppermute | solution.py:27
  108.6 11.4 %collective-permute-start.6 = (bf16[257,1024]{1,0:T(8,128)(2,1)}, bf16[257,1024]{1,0:T(8,128)(2,1)S(1)}, u32[]{:S(2)}, u32[]{:S(2)}) collective-permute-start(bf16[257,1024]{1,0:T(8,128)(2,1)} %fusion.100), channel_id=1, source_target_pairs={{0,28},{4,32},{8,36},{12,40},{16,44},{20,48},{24,52},{28,56},{32,6... | collective-permute-start | bytes 1579016 | tf_op jit(solution)/shard_map/ppermute | solution.py:20
  111.8 30.0 %collective-permute-start.4 = (bf16[257,1024]{1,0:T(8,128)(2,1)}, bf16[257,1024]{1,0:T(8,128)(2,1)S(1)}, u32[]{:S(2)}, u32[]{:S(2)}) collective-permute-start(bf16[257,1024]{1,0:T(8,128)(2,1)} %fusion.100), channel_id=1, source_target_pairs={{0,20},{4,24},{8,28},{12,32},{16,36},{20,40},{24,44},{28,48},{32,5... | collective-permute-start | bytes 1579016 | tf_op jit(solution)/shard_map/ppermute | solution.py:20
  120.0 36.0 %collective-permute-start.1 = (bf16[257,1024]{1,0:T(8,128)(2,1)}, bf16[257,1024]{1,0:T(8,128)(2,1)}, u32[]{:S(2)}, u32[]{:S(2)}) collective-permute-start(bf16[257,1024]{1,0:T(8,128)(2,1)} %fusion.100), channel_id=1, source_target_pairs={{0,8},{4,12},{8,16},{12,20},{16,24},{20,28},{24,32},{28,36},{32,40... | collective-permute-start | bytes 1579016 | tf_op jit(solution)/shard_map/ppermute | solution.py:20
  136.6 30.4 %collective-permute-start = (bf16[257,1024]{1,0:T(8,128)(2,1)}, bf16[257,1024]{1,0:T(8,128)(2,1)}, u32[]{:S(2)}, u32[]{:S(2)}) collective-permute-start(bf16[257,1024]{1,0:T(8,128)(2,1)} %fusion.100), channel_id=1, source_target_pairs={{0,4},{4,8},{8,12},{12,16},{16,20},{20,24},{24,28},{28,32},{32,36}... | collective-permute-start | bytes 1579016 | tf_op jit(solution)/shard_map/ppermute | solution.py:20
  141.9 48.2 %collective-permute-start.11 = (bf16[64,4096]{1,0:T(8,128)(2,1)}, bf16[64,4096]{1,0:T(8,128)(2,1)}, u32[]{:S(2)}, u32[]{:S(2)}) collective-permute-start(bf16[64,4096]{1,0:T(8,128)(2,1)} %maximum_select_fusion.3), channel_id=1, source_target_pairs={{0,128},{4,132},{8,136},{12,140},{16,144},{20,148},{24,152},{28,15... | collective-permute-start | bytes 1572872 | tf_op jit(solution)/shard_map/ppermute | solution.py:27
  184.8 47.7 %copy-start.47 = (pred[256,256]{0,1:T(8,128)(4,1)}, pred[256,256]{0,1:T(8,128)(4,1)S(1)}, u32[]{:S(2)}) copy-start(pred[256,256]{0,1:T(8,128)(4,1)S(1)} %get-tuple-element.76) | copy-start | bytes 196612
  184.8 48.9 %copy-start.44 = (pred[256,256]{0,1:T(8,128)(4,1)}, pred[256,256]{0,1:T(8,128)(4,1)S(1)}, u32[]{:S(2)}) copy-start(pred[256,256]{0,1:T(8,128)(4,1)S(1)} %get-tuple-element.75) | copy-start | bytes 196612
  184.8 50.2 %copy-start.41 = (pred[256,256]{0,1:T(8,128)(4,1)}, pred[256,256]{0,1:T(8,128)(4,1)S(1)}, u32[]{:S(2)}) copy-start(pred[256,256]{0,1:T(8,128)(4,1)S(1)} %get-tuple-element.74) | copy-start | bytes 196612
  184.9 51.4 %copy-start.38 = (pred[256,256]{0,1:T(8,128)(4,1)}, pred[256,256]{0,1:T(8,128)(4,1)S(1)}, u32[]{:S(2)}) copy-start(pred[256,256]{0,1:T(8,128)(4,1)S(1)} %get-tuple-element.73) | copy-start | bytes 196612
  184.9 52.6 %copy-start.35 = (pred[256,256]{0,1:T(8,128)(4,1)}, pred[256,256]{0,1:T(8,128)(4,1)S(1)}, u32[]{:S(2)}) copy-start(pred[256,256]{0,1:T(8,128)(4,1)S(1)} %get-tuple-element.72) | copy-start | bytes 196612
  184.9 55.0 %copy-start.51 = (pred[256,256]{0,1:T(8,128)(4,1)}, pred[256,256]{0,1:T(8,128)(4,1)S(1)}, u32[]{:S(2)}) copy-start(pred[256,256]{0,1:T(8,128)(4,1)S(1)} %get-tuple-element.71) | copy-start | bytes 196612
  185.7 46.8 %copy-start.10 = (f32[4,256,256]{1,2,0:T(8,128)}, f32[4,256,256]{1,2,0:T(8,128)S(1)}, u32[]{:S(2)}) copy-start(f32[4,256,256]{1,2,0:T(8,128)S(1)} %get-tuple-element.83) | copy-start | bytes 3145732
  186.1 47.7 %copy-start.8 = (f32[4,256,256]{1,2,0:T(8,128)}, f32[4,256,256]{1,2,0:T(8,128)S(1)}, u32[]{:S(2)}) copy-start(f32[4,256,256]{1,2,0:T(8,128)S(1)} %get-tuple-element.85) | copy-start | bytes 3145732
  186.5 48.5 %copy-start.6 = (f32[4,256,256]{1,2,0:T(8,128)}, f32[4,256,256]{1,2,0:T(8,128)S(1)}, u32[]{:S(2)}) copy-start(f32[4,256,256]{1,2,0:T(8,128)S(1)} %get-tuple-element.87) | copy-start | bytes 3145732
  186.9 49.4 %copy-start.4 = (f32[4,256,256]{1,2,0:T(8,128)}, f32[4,256,256]{1,2,0:T(8,128)S(1)}, u32[]{:S(2)}) copy-start(f32[4,256,256]{1,2,0:T(8,128)S(1)} %get-tuple-element.89) | copy-start | bytes 3145732
  187.3 50.1 %copy-start.2 = (f32[4,256,256]{1,2,0:T(8,128)}, f32[4,256,256]{1,2,0:T(8,128)S(1)}, u32[]{:S(2)}) copy-start(f32[4,256,256]{1,2,0:T(8,128)S(1)} %get-tuple-element.91) | copy-start | bytes 3145732
  187.7 51.0 %copy-start = (f32[4,256,256]{1,2,0:T(8,128)}, f32[4,256,256]{1,2,0:T(8,128)S(1)}, u32[]{:S(2)}) copy-start(f32[4,256,256]{1,2,0:T(8,128)S(1)} %get-tuple-element.93) | copy-start | bytes 3145732
  188.5 44.0 %copy-start.90 = (f32[4,256]{1,0:T(4,128)}, f32[4,256]{1,0:T(4,128)S(1)}, u32[]{:S(2)}) copy-start(f32[4,256]{1,0:T(4,128)S(1)} %get-tuple-element.43) | copy-start | bytes 12292
  188.5 45.2 %copy-start.91 = (f32[4,256]{1,0:T(4,128)}, f32[4,256]{1,0:T(4,128)S(1)}, u32[]{:S(2)}) copy-start(f32[4,256]{1,0:T(4,128)S(1)} %get-tuple-element.44) | copy-start | bytes 12292
  188.5 46.5 %copy-start.92 = (f32[4,256]{1,0:T(4,128)}, f32[4,256]{1,0:T(4,128)S(1)}, u32[]{:S(2)}) copy-start(f32[4,256]{1,0:T(4,128)S(1)} %get-tuple-element.45) | copy-start | bytes 12292
  188.5 47.7 %copy-start.93 = (f32[4,256]{1,0:T(4,128)}, f32[4,256]{1,0:T(4,128)S(1)}, u32[]{:S(2)}) copy-start(f32[4,256]{1,0:T(4,128)S(1)} %get-tuple-element.46) | copy-start | bytes 12292
  188.5 48.9 %copy-start.94 = (f32[4,256]{1,0:T(4,128)}, f32[4,256]{1,0:T(4,128)S(1)}, u32[]{:S(2)}) copy-start(f32[4,256]{1,0:T(4,128)S(1)} %get-tuple-element.47) | copy-start | bytes 12292
  188.6 50.1 %copy-start.95 = (f32[4,256]{1,0:T(4,128)}, f32[4,256]{1,0:T(4,128)S(1)}, u32[]{:S(2)}) copy-start(f32[4,256]{1,0:T(4,128)S(1)} %get-tuple-element.48) | copy-start | bytes 12292
  191.9 39.2 %collective-permute-start.12 = (bf16[128,4096]{1,0:T(8,128)(2,1)S(1)}, bf16[128,4096]{1,0:T(8,128)(2,1)S(1)}, u32[]{:S(2)}, u32[]{:S(2)}) collective-permute-start(bf16[128,4096]{1,0:T(8,128)(2,1)S(1)} %maximum_select_fusion.2), channel_id=1, source_target_pairs={{0,16},{4,20},{8,24},{12,28},{16,0},{20,4},{24,8},{28,12},{32,48},... | collective-permute-start | bytes 3145736 | tf_op jit(solution)/shard_map/ppermute | solution.py:27
  231.7 46.2 %collective-permute-start.13 = (bf16[256,4096]{1,0:T(8,128)(2,1)S(1)}, bf16[256,4096]{1,0:T(8,128)(2,1)S(1)}, u32[]{:S(2)}, u32[]{:S(2)}) collective-permute-start(bf16[256,4096]{1,0:T(8,128)(2,1)S(1)} %maximum_select_fusion.1), channel_id=1, source_target_pairs={{0,4},{4,0},{8,12},{12,8},{16,20},{20,16},{24,28},{28,24},{32,36},... | collective-permute-start | bytes 6291464 | tf_op jit(solution)/shard_map/ppermute | solution.py:27
  293.7 258.5 %reduce-scatter.6.cloned.1.call-start = ((), (), s32[]{:S(2)}) async-start(), calls=%async_computation.5 | async-start | bytes 1310720 | tf_op jit(solution)/shard_map/reduce_scatter | solution.py:113
  320.5 174.5 %collective-permute-start.21 = (bf16[256,1024]{1,0:T(8,128)(2,1)}, bf16[256,1024]{1,0:T(8,128)(2,1)}, u32[]{:S(2)}, u32[]{:S(2)}) collective-permute-start(bf16[256,1024]{1,0:T(8,128)(2,1)} %pad_maximum_fusion.7), channel_id=1, source_target_pairs={{32,0},{36,4},{40,8},{44,12},{48,16},{52,20},{56,24},{60,28},{64,3... | collective-permute-start | bytes 1572872 | tf_op jit(solution)/shard_map/ppermute | solution.py:20
  331.8 164.5 %collective-permute-start.20 = (bf16[256,1024]{1,0:T(8,128)(2,1)}, bf16[256,1024]{1,0:T(8,128)(2,1)}, u32[]{:S(2)}, u32[]{:S(2)}) collective-permute-start(bf16[256,1024]{1,0:T(8,128)(2,1)} %pad_maximum_fusion.6), channel_id=1, source_target_pairs={{28,0},{32,4},{36,8},{40,12},{44,16},{48,20},{52,24},{56,28},{60,3... | collective-permute-start | bytes 1572872 | tf_op jit(solution)/shard_map/ppermute | solution.py:20
  343.0 154.6 %collective-permute-start.19 = (bf16[256,1024]{1,0:T(8,128)(2,1)}, bf16[256,1024]{1,0:T(8,128)(2,1)}, u32[]{:S(2)}, u32[]{:S(2)}) collective-permute-start(bf16[256,1024]{1,0:T(8,128)(2,1)} %pad_maximum_fusion.5), channel_id=1, source_target_pairs={{24,0},{28,4},{32,8},{36,12},{40,16},{44,20},{48,24},{52,28},{56,3... | collective-permute-start | bytes 1572872 | tf_op jit(solution)/shard_map/ppermute | solution.py:20
  354.3 201.8 %collective-permute-start.18 = (bf16[256,1024]{1,0:T(8,128)(2,1)}, bf16[256,1024]{1,0:T(8,128)(2,1)}, u32[]{:S(2)}, u32[]{:S(2)}) collective-permute-start(bf16[256,1024]{1,0:T(8,128)(2,1)} %pad_maximum_fusion.4), channel_id=1, source_target_pairs={{20,0},{24,4},{28,8},{32,12},{36,16},{40,20},{44,24},{48,28},{52,3... | collective-permute-start | bytes 1572872 | tf_op jit(solution)/shard_map/ppermute | solution.py:20
  357.9 118.9 %copy-start.37 = (pred[256,256]{0,1:T(8,128)(4,1)S(1)}, pred[256,256]{0,1:T(8,128)(4,1)}, u32[]{:S(2)}) copy-start(pred[256,256]{0,1:T(8,128)(4,1)} %copy-done.35) | copy-start | bytes 196612
  365.5 191.8 %collective-permute-start.17 = (bf16[256,1024]{1,0:T(8,128)(2,1)}, bf16[256,1024]{1,0:T(8,128)(2,1)}, u32[]{:S(2)}, u32[]{:S(2)}) collective-permute-start(bf16[256,1024]{1,0:T(8,128)(2,1)} %pad_maximum_fusion.3), channel_id=1, source_target_pairs={{16,0},{20,4},{24,8},{28,12},{32,16},{36,20},{40,24},{44,28},{48,3... | collective-permute-start | bytes 1572872 | tf_op jit(solution)/shard_map/ppermute | solution.py:20
  476.5 92.4 %reduce-scatter.8.cloned.1.call-start = ((), (), s32[]{:S(2)}) async-start(), calls=%async_computation.6 | async-start | bytes 393216 | tf_op jit(solution)/shard_map/reduce_scatter | solution.py:113
  495.0 63.5 %collective-permute-start.16 = (bf16[256,1024]{1,0:T(8,128)(2,1)}, bf16[256,1024]{1,0:T(8,128)(2,1)}, u32[]{:S(2)}, u32[]{:S(2)}) collective-permute-start(bf16[256,1024]{1,0:T(8,128)(2,1)} %pad_maximum_fusion.2), channel_id=1, source_target_pairs={{12,0},{16,4},{20,8},{24,12},{28,16},{32,20},{36,24},{40,28},{44,3... | collective-permute-start | bytes 1572872 | tf_op jit(solution)/shard_map/ppermute | solution.py:20
  496.3 63.3 %collective-permute-start.15 = (bf16[256,1024]{1,0:T(8,128)(2,1)}, bf16[256,1024]{1,0:T(8,128)(2,1)}, u32[]{:S(2)}, u32[]{:S(2)}) collective-permute-start(bf16[256,1024]{1,0:T(8,128)(2,1)} %pad_maximum_fusion.1), channel_id=1, source_target_pairs={{8,0},{12,4},{16,8},{20,12},{24,16},{28,20},{32,24},{36,28},{40,32... | collective-permute-start | bytes 1572872 | tf_op jit(solution)/shard_map/ppermute | solution.py:20
  497.6 63.2 %collective-permute-start.14 = (bf16[256,1024]{1,0:T(8,128)(2,1)}, bf16[256,1024]{1,0:T(8,128)(2,1)}, u32[]{:S(2)}, u32[]{:S(2)}) collective-permute-start(bf16[256,1024]{1,0:T(8,128)(2,1)} %pad_maximum_fusion), channel_id=1, source_target_pairs={{4,0},{8,4},{12,8},{16,12},{20,16},{24,20},{28,24},{32,28},{36,32}... | collective-permute-start | bytes 1572872 | tf_op jit(solution)/shard_map/ppermute | solution.py:20
  (92 other events, 877.1 us)
Sparse Core Ops, SparseCore 0:
  31.4 62.7 all-gather.1
  293.8 182.6 reduce-scatter.3
  479.1 73.0 reduce-scatter.5
  555.0 13.8 reduce-scatter.7

commit v3 on v2

--- a/solution.py
+++ b/solution.py
@@ -48,8 +48,6 @@
         query_heads = query.reshape(tok_rows, head_count, DH)
 
         grad_full = lax.all_gather(grad_out, FS, axis=1, tiled=True)
-        weight_rows = gathered_rows(out_weight, cycle_index, devices)
-
         key_value = jnp.concatenate([key, value], axis=1)
         doc_row = jnp.zeros((1, 2 * feature_width), jnp.bfloat16)
         doc_row = doc_row.at[0, :tok_rows].set(own_docs.astype(jnp.bfloat16))
@@ -109,9 +107,12 @@
             .transpose(1, 2, 0, 3, 4)
             .reshape(partial_weight.shape)
         )
+        weight_local, partial_weight = lax.optimization_barrier((out_weight, partial_weight))
         for axis in ("cz", "cx", "cy"):
             partial_weight = lax.psum_scatter(partial_weight, axis, scatter_dimension=0, tiled=True)
         grad_weight = partial_weight
+
+        weight_rows = gathered_rows(weight_local, cycle_index, devices)
 
         grad_attn = lax.dot_general(
             grad_full,

time: 587 us -> 534 us (0.910)
  the two profiles are of different devices: /device:TPU:1 before, /device:TPU:8 now
where the time goes in v3:
time: 534 us; the launch traced here: 528 us
  waiting for transfers between devices  230 us (43%)
  starting transfers between devices  122 us (23%)
  local copies, waits for them, and re-layouts  63.1 us (12%)
  other arithmetic  51.8 us (10%)
  matrix products  44.7 us (8%)
  between operations  16.1 us (3%)
    ppermute x6, waiting for transfers between devices, gathered_rows(): other = lax.ppermute(block, CTX, [(i, i ^ bit) for i in range(devices)])  110 us
    ppermute x16, starting transfers between devices, shifted_by(): return lax.ppermute(array, CTX, pairs)  109 us
    ppermute x16, waiting for transfers between devices, shifted_by(): return lax.ppermute(array, CTX, pairs)  101 us
    slice x16, local copies, waits for them, and re-layouts, shards(): blocks.append((got[:, :feature_width], got[:, feature_width:], got_docs))  20.4 us
    reduce_scatter x3, waiting for transfers between devices, shards(): lax.psum_scatter(partial_weight, axis, scatter_dimension=0, tiled=True)  18.8 us
    concatenate x8, other arithmetic, shards(): sent = jnp.concatenate([key_part, value_part], axis=1).astype(jnp.bfloat16)  15 us
    unnamed x203, local copies, waits for them, and re-layouts  14.9 us
    ppermute x6, starting transfers between devices, gathered_rows(): other = lax.ppermute(block, CTX, [(i, i ^ bit) for i in range(devices)])  13.2 us
  transfers between devices with their start and end apart: 26, of which 11 were waited for; matrix products, arithmetic and copies ran while one was open for 26% of the time, Pallas kernels for 0%

profile of v3, /device:TPU:8, one launch (start us, length us, event | category | flops | bytes accessed | tf_op | source)
XLA Modules:
  0.0 527.5 jit_solution(5194477727232424082)
XLA Ops:
  9.2 1.9 fusion.100
  11.1 3.8 collective-permute-start.3
  14.9 4.8 collective-permute-start.4
  19.7 6.0 %collective-permute-start.5 = (bf16[257,1024]{1,0:T(8,128)(2,1)}, bf16[257,1024]{1,0:T(8,128)(2,1)S(1)}, u32[]{:S(2)}, u32[]{:S(2)}) collective-permute-start(bf16[257,1024]{1,0:T(8,128)(2,1)} %fusion.100), channel_id=1, source_target_pairs={{0,24},{4,28},{8,32},{12,36},{16,40},{20,44},{24,48},{28,52},{32,5... | collective-permute-start | bytes 1579016 | tf_op jit(solution)/shard_map/ppermute | solution.py:20
  25.7 4.3 collective-permute-start
  30.0 5.3 collective-permute-start.2
  39.1 31.6 %collective-permute-done.2 = bf16[257,1024]{1,0:T(8,128)(2,1)S(1)} collective-permute-done((bf16[257,1024]{1,0:T(8,128)(2,1)}, bf16[257,1024]{1,0:T(8,128)(2,1)S(1)}, u32[]{:S(2)}, u32[]{:S(2)}) %collective-permute-start.2) | collective-permute-done | bytes 526368 | tf_op jit(solution)/shard_map/ppermute | solution.py:20
  70.7 43.5 %collective-permute-start.6 = (bf16[257,1024]{1,0:T(8,128)(2,1)}, bf16[257,1024]{1,0:T(8,128)(2,1)}, u32[]{:S(2)}, u32[]{:S(2)}) collective-permute-start(bf16[257,1024]{1,0:T(8,128)(2,1)} %fusion.100), channel_id=1, source_target_pairs={{0,28},{4,32},{8,36},{12,40},{16,44},{20,48},{24,52},{28,56},{32,6... | collective-permute-start | bytes 1579016 | tf_op jit(solution)/shard_map/ppermute | solution.py:20
  114.3 8.2 %collective-permute-start.7 = (bf16[257,1024]{1,0:T(8,128)(2,1)}, bf16[257,1024]{1,0:T(8,128)(2,1)}, u32[]{:S(2)}, u32[]{:S(2)}) collective-permute-start(bf16[257,1024]{1,0:T(8,128)(2,1)} %fusion.100), channel_id=1, source_target_pairs={{0,32},{4,36},{8,40},{12,44},{16,48},{20,52},{24,56},{28,60},{32,6... | collective-permute-start | bytes 1579016 | tf_op jit(solution)/shard_map/ppermute | solution.py:20
  124.4 1.9 collective-permute-start.1
  128.5 1.9 fusion.244
  132.1 42.1 %collective-permute-done.1 = bf16[257,1024]{1,0:T(8,128)(2,1)} collective-permute-done((bf16[257,1024]{1,0:T(8,128)(2,1)}, bf16[257,1024]{1,0:T(8,128)(2,1)}, u32[]{:S(2)}, u32[]{:S(2)}) %collective-permute-start.1) | collective-permute-done | bytes 526368 | tf_op jit(solution)/shard_map/ppermute | solution.py:20
  176.1 1.9 fusion.247
  179.2 1.9 fusion.248
  185.6 1.9 copy.397
  210.5 2.9 convolution_bitcast_fusion
  213.4 3.9 copy.407
  218.2 2.4 collective-permute-start.8
  220.6 5.8 %collective-permute-done.8 = bf16[8,4096]{1,0:T(8,128)(2,1)S(1)} collective-permute-done((bf16[8,4096]{1,0:T(8,128)(2,1)S(1)}, bf16[8,4096]{1,0:T(8,128)(2,1)S(1)}, u32[]{:S(2)}, u32[]{:S(2)}) %collective-permute-start.8) | collective-permute-done | bytes 65568 | tf_op jit(solution)/shard_map/ppermute | solution.py:27
  226.7 6.0 %collective-permute-done.9 = bf16[16,4096]{1,0:T(8,128)(2,1)S(1)} collective-permute-done((bf16[16,4096]{1,0:T(8,128)(2,1)S(1)}, bf16[16,4096]{1,0:T(8,128)(2,1)S(1)}, u32[]{:S(2)}, u32[]{:S(2)}) %collective-permute-start.9) | collective-permute-done | bytes 131104 | tf_op jit(solution)/shard_map/ppermute | solution.py:27
  232.8 7.9 %collective-permute-done.10 = bf16[32,4096]{1,0:T(8,128)(2,1)S(1)} collective-permute-done((bf16[32,4096]{1,0:T(8,128)(2,1)S(1)}, bf16[32,4096]{1,0:T(8,128)(2,1)S(1)}, u32[]{:S(2)}, u32[]{:S(2)}) %collective-permute-start.10) | collective-permute-done | bytes 262176 | tf_op jit(solution)/shard_map/ppermute | solution.py:27
  241.6 8.6 %collective-permute-done.11 = bf16[64,4096]{1,0:T(8,128)(2,1)} collective-permute-done((bf16[64,4096]{1,0:T(8,128)(2,1)S(1)}, bf16[64,4096]{1,0:T(8,128)(2,1)}, u32[]{:S(2)}, u32[]{:S(2)}) %collective-permute-start.11) | collective-permute-done | bytes 524320 | tf_op jit(solution)/shard_map/ppermute | solution.py:27
  251.9 5.1 collective-permute-start.12
  257.0 43.5 %collective-permute-done.12 = bf16[128,4096]{1,0:T(8,128)(2,1)} collective-permute-done((bf16[128,4096]{1,0:T(8,128)(2,1)S(1)}, bf16[128,4096]{1,0:T(8,128)(2,1)}, u32[]{:S(2)}, u32[]{:S(2)}) %collective-permute-start.12) | collective-permute-done | bytes 1048608 | tf_op jit(solution)/shard_map/ppermute | solution.py:27
  300.6 3.7 maximum_select_fusion.1
  304.3 5.2 collective-permute-start.13
  310.3 38.6 %collective-permute-done.13 = bf16[256,4096]{1,0:T(8,128)(2,1)} collective-permute-done((bf16[256,4096]{1,0:T(8,128)(2,1)}, bf16[256,4096]{1,0:T(8,128)(2,1)}, u32[]{:S(2)}, u32[]{:S(2)}) %collective-permute-start.13) | collective-permute-done | bytes 2097184 | tf_op jit(solution)/shard_map/ppermute | solution.py:27
  348.9 4.6 maximum_select_fusion
  359.3 2.0 pad_maximum_fusion
  361.3 1.9 collective-permute-start.14
  363.2 2.4 fusion.118
  365.6 2.0 copy.490
  377.0 4.4 collective-permute-start.15
  388.0 1.9 pad_maximum_fusion.2
  390.0 1.9 collective-permute-start.16
  401.3 3.6 collective-permute-start.17
  411.6 1.9 pad_maximum_fusion.4
  413.5 5.4 %collective-permute-start.18 = (bf16[256,1024]{1,0:T(8,128)(2,1)}, bf16[256,1024]{1,0:T(8,128)(2,1)}, u32[]{:S(2)}, u32[]{:S(2)}) collective-permute-start(bf16[256,1024]{1,0:T(8,128)(2,1)} %pad_maximum_fusion.4), channel_id=1, source_target_pairs={{20,0},{24,4},{28,8},{32,12},{36,16},{40,20},{44,24},{48,28},{52,3... | collective-permute-start | bytes 1572872 | tf_op jit(solution)/shard_map/ppermute | solution.py:20
  426.8 2.3 convolution_convert_fusion.1
  433.3 1.9 pad_maximum_fusion.5
  435.1 1.9 pad_maximum_fusion.6
  438.1 2.1 fusion.60
  449.5 8.1 %collective-permute-start.19 = (bf16[256,1024]{1,0:T(8,128)(2,1)}, bf16[256,1024]{1,0:T(8,128)(2,1)S(1)}, u32[]{:S(2)}, u32[]{:S(2)}) collective-permute-start(bf16[256,1024]{1,0:T(8,128)(2,1)} %pad_maximum_fusion.5), channel_id=1, source_target_pairs={{24,0},{28,4},{32,8},{36,12},{40,16},{44,20},{48,24},{52,28},{56,3... | collective-permute-start | bytes 1572872 | tf_op jit(solution)/shard_map/ppermute | solution.py:20
  457.6 3.5 collective-permute-start.20
  461.1 1.9 collective-permute-start.21
  463.4 18.8 %reduce-scatter.6.cloned.1.call-done = f32[16,4096]{1,0:T(8,128)} async-done(((f32[64,4096]{1,0:T(8,128)}), f32[16,4096]{1,0:T(8,128)}) %reduce-scatter.6.cloned.1.call-update) | async-done | bytes 262160 | tf_op jit(solution)/shard_map/reduce_scatter | solution.py:112
  489.5 6.0 %collective-permute-done.20 = bf16[256,1024]{1,0:T(8,128)(2,1)} collective-permute-done((bf16[256,1024]{1,0:T(8,128)(2,1)}, bf16[256,1024]{1,0:T(8,128)(2,1)}, u32[]{:S(2)}, u32[]{:S(2)}) %collective-permute-start.20) | collective-permute-done | bytes 524320 | tf_op jit(solution)/shard_map/ppermute | solution.py:20
  496.7 20.9 %collective-permute-done.21 = bf16[256,1024]{1,0:T(8,128)(2,1)} collective-permute-done((bf16[256,1024]{1,0:T(8,128)(2,1)}, bf16[256,1024]{1,0:T(8,128)(2,1)}, u32[]{:S(2)}, u32[]{:S(2)}) %collective-permute-start.21) | collective-permute-done | bytes 524320 | tf_op jit(solution)/shard_map/ppermute | solution.py:20
  (359 shorter events, 117.4 us)
Async XLA Ops:
  7.2 31.8 %copy-start.79 = (bf16[256,512]{1,0:T(8,128)(2,1)S(1)}, bf16[256,512]{1,0:T(8,128)(2,1)}, u32[]{:S(2)}) copy-start(bf16[256,512]{1,0:T(8,128)(2,1)} %param.8) | copy-start | bytes 786436
  7.2 203.3 %all-gather.2.cloned.1.call-start = ((), (), s32[]{:S(2)}) async-start(), calls=%async_computation.3 | async-start | bytes 2621440 | tf_op jit(solution)/shard_map/all_gather | solution.py:50
  11.1 117.4 %collective-permute-start.3 = (bf16[257,1024]{1,0:T(8,128)(2,1)}, bf16[257,1024]{1,0:T(8,128)(2,1)}, u32[]{:S(2)}, u32[]{:S(2)}) collective-permute-start(bf16[257,1024]{1,0:T(8,128)(2,1)} %fusion.100), channel_id=1, source_target_pairs={{0,16},{4,20},{8,24},{12,28},{16,32},{20,36},{24,40},{28,44},{32,4... | collective-permute-start | bytes 1579016 | tf_op jit(solution)/shard_map/ppermute | solution.py:20
  14.9 112.5 %collective-permute-start.4 = (bf16[257,1024]{1,0:T(8,128)(2,1)}, bf16[257,1024]{1,0:T(8,128)(2,1)}, u32[]{:S(2)}, u32[]{:S(2)}) collective-permute-start(bf16[257,1024]{1,0:T(8,128)(2,1)} %fusion.100), channel_id=1, source_target_pairs={{0,20},{4,24},{8,28},{12,32},{16,36},{20,40},{24,44},{28,48},{32,5... | collective-permute-start | bytes 1579016 | tf_op jit(solution)/shard_map/ppermute | solution.py:20
  19.7 103.9 %collective-permute-start.5 = (bf16[257,1024]{1,0:T(8,128)(2,1)}, bf16[257,1024]{1,0:T(8,128)(2,1)S(1)}, u32[]{:S(2)}, u32[]{:S(2)}) collective-permute-start(bf16[257,1024]{1,0:T(8,128)(2,1)} %fusion.100), channel_id=1, source_target_pairs={{0,24},{4,28},{8,32},{12,36},{16,40},{20,44},{24,48},{28,52},{32,5... | collective-permute-start | bytes 1579016 | tf_op jit(solution)/shard_map/ppermute | solution.py:20
  25.7 88.6 %collective-permute-start = (bf16[257,1024]{1,0:T(8,128)(2,1)}, bf16[257,1024]{1,0:T(8,128)(2,1)}, u32[]{:S(2)}, u32[]{:S(2)}) collective-permute-start(bf16[257,1024]{1,0:T(8,128)(2,1)} %fusion.100), channel_id=1, source_target_pairs={{0,4},{4,8},{8,12},{12,16},{16,20},{20,24},{24,28},{28,32},{32,36}... | collective-permute-start | bytes 1579016 | tf_op jit(solution)/shard_map/ppermute | solution.py:20
  30.0 40.6 %collective-permute-start.2 = (bf16[257,1024]{1,0:T(8,128)(2,1)}, bf16[257,1024]{1,0:T(8,128)(2,1)S(1)}, u32[]{:S(2)}, u32[]{:S(2)}) collective-permute-start(bf16[257,1024]{1,0:T(8,128)(2,1)} %fusion.100), channel_id=1, source_target_pairs={{0,12},{4,16},{8,20},{12,24},{16,28},{20,32},{24,36},{28,40},{32,4... | collective-permute-start | bytes 1579016 | tf_op jit(solution)/shard_map/ppermute | solution.py:20
  35.4 406.7 %reduce-scatter.4.cloned.1.call-start = ((), (), s32[]{:S(2)}) async-start(), calls=%async_computation.4 | async-start | bytes 9437184 | tf_op jit(solution)/shard_map/reduce_scatter | solution.py:112
  39.0 164.1 %copy-start.26 = (bf16[256,512]{0,1:T(8,128)(2,1)}, bf16[256,512]{0,1:T(8,128)(2,1)S(1)}, u32[]{:S(2)}) copy-start(bf16[256,512]{0,1:T(8,128)(2,1)S(1)} %copy.578) | copy-start | bytes 786436
  70.7 43.6 %copy-start.73 = (bf16[257,1024]{1,0:T(8,128)(2,1)}, bf16[257,1024]{1,0:T(8,128)(2,1)S(1)}, u32[]{:S(2)}) copy-start(bf16[257,1024]{1,0:T(8,128)(2,1)S(1)} %collective-permute-done.2) | copy-start | bytes 1579012
  70.7 105.4 %collective-permute-start.6 = (bf16[257,1024]{1,0:T(8,128)(2,1)}, bf16[257,1024]{1,0:T(8,128)(2,1)}, u32[]{:S(2)}, u32[]{:S(2)}) collective-permute-start(bf16[257,1024]{1,0:T(8,128)(2,1)} %fusion.100), channel_id=1, source_target_pairs={{0,28},{4,32},{8,36},{12,40},{16,44},{20,48},{24,52},{28,56},{32,6... | collective-permute-start | bytes 1579016 | tf_op jit(solution)/shard_map/ppermute | solution.py:20
  114.3 64.9 %collective-permute-start.7 = (bf16[257,1024]{1,0:T(8,128)(2,1)}, bf16[257,1024]{1,0:T(8,128)(2,1)}, u32[]{:S(2)}, u32[]{:S(2)}) collective-permute-start(bf16[257,1024]{1,0:T(8,128)(2,1)} %fusion.100), channel_id=1, source_target_pairs={{0,32},{4,36},{8,40},{12,44},{16,48},{20,52},{24,56},{28,60},{32,6... | collective-permute-start | bytes 1579016 | tf_op jit(solution)/shard_map/ppermute | solution.py:20
  124.4 49.8 %collective-permute-start.1 = (bf16[257,1024]{1,0:T(8,128)(2,1)}, bf16[257,1024]{1,0:T(8,128)(2,1)}, u32[]{:S(2)}, u32[]{:S(2)}) collective-permute-start(bf16[257,1024]{1,0:T(8,128)(2,1)} %fusion.100), channel_id=1, source_target_pairs={{0,8},{4,12},{8,16},{12,20},{16,24},{20,28},{24,32},{28,36},{32,40... | collective-permute-start | bytes 1579016 | tf_op jit(solution)/shard_map/ppermute | solution.py:20
  130.5 69.4 %copy-start.36 = (bf16[256,512]{0,1:T(8,128)(2,1)}, bf16[256,512]{0,1:T(8,128)(2,1)S(1)}, u32[]{:S(2)}) copy-start(bf16[256,512]{0,1:T(8,128)(2,1)S(1)} %copy.572) | copy-start | bytes 786436
  130.6 69.7 %copy-start.38 = (bf16[256,512]{0,1:T(8,128)(2,1)}, bf16[256,512]{0,1:T(8,128)(2,1)S(1)}, u32[]{:S(2)}) copy-start(bf16[256,512]{0,1:T(8,128)(2,1)S(1)} %copy.570) | copy-start | bytes 786436
  130.8 69.9 %copy-start.28 = (bf16[256,512]{0,1:T(8,128)(2,1)}, bf16[256,512]{0,1:T(8,128)(2,1)S(1)}, u32[]{:S(2)}) copy-start(bf16[256,512]{0,1:T(8,128)(2,1)S(1)} %copy.575) | copy-start | bytes 786436
  130.9 70.2 %copy-start.30 = (bf16[256,512]{0,1:T(8,128)(2,1)}, bf16[256,512]{0,1:T(8,128)(2,1)S(1)}, u32[]{:S(2)}) copy-start(bf16[256,512]{0,1:T(8,128)(2,1)S(1)} %copy.574) | copy-start | bytes 786436
  132.1 69.4 %copy-start.31 = (bf16[256,512]{0,1:T(8,128)(2,1)}, bf16[256,512]{0,1:T(8,128)(2,1)S(1)}, u32[]{:S(2)}) copy-start(bf16[256,512]{0,1:T(8,128)(2,1)S(1)} %copy.573) | copy-start | bytes 786436
  176.1 25.8 %copy-start.40 = (bf16[256,512]{0,1:T(8,128)(2,1)}, bf16[256,512]{0,1:T(8,128)(2,1)S(1)}, u32[]{:S(2)}) copy-start(bf16[256,512]{0,1:T(8,128)(2,1)S(1)} %copy.571) | copy-start | bytes 786436
  179.2 23.2 %copy-start.32 = (bf16[256,512]{0,1:T(8,128)(2,1)}, bf16[256,512]{0,1:T(8,128)(2,1)S(1)}, u32[]{:S(2)}) copy-start(bf16[256,512]{0,1:T(8,128)(2,1)S(1)} %copy.576) | copy-start | bytes 786436
  199.9 9.3 %copy-start.70 = (pred[256,256]{0,1:T(8,128)(4,1)}, pred[256,256]{0,1:T(8,128)(4,1)S(1)}, u32[]{:S(2)}) copy-start(pred[256,256]{0,1:T(8,128)(4,1)S(1)} %get-tuple-element.75) | copy-start | bytes 196612
  217.4 264.9 %reduce-scatter.6.cloned.1.call-start = ((), (), s32[]{:S(2)}) async-start(), calls=%async_computation.5 | async-start | bytes 1310720 | tf_op jit(solution)/shard_map/reduce_scatter | solution.py:112
  218.2 8.2 %collective-permute-start.8 = (bf16[8,4096]{1,0:T(8,128)(2,1)S(1)}, bf16[8,4096]{1,0:T(8,128)(2,1)S(1)}, u32[]{:S(2)}, u32[]{:S(2)}) collective-permute-start(bf16[8,4096]{1,0:T(8,128)(2,1)S(1)} %copy-done.80), channel_id=1, source_target_pairs={{0,64},{4,68},{8,72},{12,76},{16,80},{20,84},{24,88},{28,92},{32,9... | collective-permute-start | bytes 196616 | tf_op jit(solution)/shard_map/ppermute | solution.py:27
  226.4 6.3 %collective-permute-start.9 = (bf16[16,4096]{1,0:T(8,128)(2,1)S(1)}, bf16[16,4096]{1,0:T(8,128)(2,1)S(1)}, u32[]{:S(2)}, u32[]{:S(2)}) collective-permute-start(bf16[16,4096]{1,0:T(8,128)(2,1)S(1)} %maximum_select_fusion.5), channel_id=1, source_target_pairs={{0,32},{4,36},{8,40},{12,44},{16,48},{20,52},{24,56},{28,60},{32,0... | collective-permute-start | bytes 393224 | tf_op jit(solution)/shard_map/ppermute | solution.py:27
  232.7 8.0 %collective-permute-start.10 = (bf16[32,4096]{1,0:T(8,128)(2,1)S(1)}, bf16[32,4096]{1,0:T(8,128)(2,1)S(1)}, u32[]{:S(2)}, u32[]{:S(2)}) collective-permute-start(bf16[32,4096]{1,0:T(8,128)(2,1)S(1)} %maximum_select_fusion.4), channel_id=1, source_target_pairs={{0,8},{4,12},{8,0},{12,4},{16,24},{20,28},{24,16},{28,20},{32,40},... | collective-permute-start | bytes 786440 | tf_op jit(solution)/shard_map/ppermute | solution.py:27
  240.8 9.4 %collective-permute-start.11 = (bf16[64,4096]{1,0:T(8,128)(2,1)S(1)}, bf16[64,4096]{1,0:T(8,128)(2,1)}, u32[]{:S(2)}, u32[]{:S(2)}) collective-permute-start(bf16[64,4096]{1,0:T(8,128)(2,1)S(1)} %maximum_select_fusion.3), channel_id=1, source_target_pairs={{0,128},{4,132},{8,136},{12,140},{16,144},{20,148},{24,152},{28,15... | collective-permute-start | bytes 1572872 | tf_op jit(solution)/shard_map/ppermute | solution.py:27
  251.9 48.7 %collective-permute-start.12 = (bf16[128,4096]{1,0:T(8,128)(2,1)S(1)}, bf16[128,4096]{1,0:T(8,128)(2,1)}, u32[]{:S(2)}, u32[]{:S(2)}) collective-permute-start(bf16[128,4096]{1,0:T(8,128)(2,1)S(1)} %maximum_select_fusion.2), channel_id=1, source_target_pairs={{0,16},{4,20},{8,24},{12,28},{16,0},{20,4},{24,8},{28,12},{32,48},... | collective-permute-start | bytes 3145736 | tf_op jit(solution)/shard_map/ppermute | solution.py:27
  304.3 44.6 %collective-permute-start.13 = (bf16[256,4096]{1,0:T(8,128)(2,1)}, bf16[256,4096]{1,0:T(8,128)(2,1)}, u32[]{:S(2)}, u32[]{:S(2)}) collective-permute-start(bf16[256,4096]{1,0:T(8,128)(2,1)} %maximum_select_fusion.1), channel_id=1, source_target_pairs={{0,4},{4,0},{8,12},{12,8},{16,20},{20,16},{24,28},{28,24},{32,36},... | collective-permute-start | bytes 6291464 | tf_op jit(solution)/shard_map/ppermute | solution.py:27
  361.3 88.2 %collective-permute-start.14 = (bf16[256,1024]{1,0:T(8,128)(2,1)}, bf16[256,1024]{1,0:T(8,128)(2,1)}, u32[]{:S(2)}, u32[]{:S(2)}) collective-permute-start(bf16[256,1024]{1,0:T(8,128)(2,1)} %pad_maximum_fusion), channel_id=1, source_target_pairs={{4,0},{8,4},{12,8},{16,12},{20,16},{24,20},{28,24},{32,28},{36,32}... | collective-permute-start | bytes 1572872 | tf_op jit(solution)/shard_map/ppermute | solution.py:20
  370.5 10.9 %copy-start.9 = (f32[4,256,256]{1,2,0:T(8,128)S(1)}, f32[4,256,256]{1,2,0:T(8,128)}, u32[]{:S(2)}) copy-start(f32[4,256,256]{1,2,0:T(8,128)} %copy-done.8) | copy-start | bytes 3145732
  370.5 10.9 %copy-start.57 = (pred[256,256]{0,1:T(8,128)(4,1)S(1)}, pred[256,256]{0,1:T(8,128)(4,1)}, u32[]{:S(2)}) copy-start(pred[256,256]{0,1:T(8,128)(4,1)} %copy-done.56) | copy-start | bytes 196612
  377.0 80.6 %collective-permute-start.15 = (bf16[256,1024]{1,0:T(8,128)(2,1)}, bf16[256,1024]{1,0:T(8,128)(2,1)}, u32[]{:S(2)}, u32[]{:S(2)}) collective-permute-start(bf16[256,1024]{1,0:T(8,128)(2,1)} %pad_maximum_fusion.1), channel_id=1, source_target_pairs={{8,0},{12,4},{16,8},{20,12},{24,16},{28,20},{32,24},{36,28},{40,32... | collective-permute-start | bytes 1572872 | tf_op jit(solution)/shard_map/ppermute | solution.py:20
  390.0 71.1 %collective-permute-start.16 = (bf16[256,1024]{1,0:T(8,128)(2,1)}, bf16[256,1024]{1,0:T(8,128)(2,1)}, u32[]{:S(2)}, u32[]{:S(2)}) collective-permute-start(bf16[256,1024]{1,0:T(8,128)(2,1)} %pad_maximum_fusion.2), channel_id=1, source_target_pairs={{12,0},{16,4},{20,8},{24,12},{28,16},{32,20},{36,24},{40,28},{44,3... | collective-permute-start | bytes 1572872 | tf_op jit(solution)/shard_map/ppermute | solution.py:20
  394.8 10.2 %copy-start.5 = (f32[4,256,256]{1,2,0:T(8,128)S(1)}, f32[4,256,256]{1,2,0:T(8,128)}, u32[]{:S(2)}) copy-start(f32[4,256,256]{1,2,0:T(8,128)} %copy-done.4) | copy-start | bytes 3145732
  394.8 10.2 %copy-start.53 = (pred[256,256]{0,1:T(8,128)(4,1)S(1)}, pred[256,256]{0,1:T(8,128)(4,1)}, u32[]{:S(2)}) copy-start(pred[256,256]{0,1:T(8,128)(4,1)} %copy-done.52) | copy-start | bytes 196612
  401.3 85.8 %collective-permute-start.17 = (bf16[256,1024]{1,0:T(8,128)(2,1)}, bf16[256,1024]{1,0:T(8,128)(2,1)}, u32[]{:S(2)}, u32[]{:S(2)}) collective-permute-start(bf16[256,1024]{1,0:T(8,128)(2,1)} %pad_maximum_fusion.3), channel_id=1, source_target_pairs={{16,0},{20,4},{24,8},{28,12},{32,16},{36,20},{40,24},{44,28},{48,3... | collective-permute-start | bytes 1572872 | tf_op jit(solution)/shard_map/ppermute | solution.py:20
  406.2 12.8 %copy-start.1 = (f32[4,256,256]{1,2,0:T(8,128)S(1)}, f32[4,256,256]{1,2,0:T(8,128)}, u32[]{:S(2)}) copy-start(f32[4,256,256]{1,2,0:T(8,128)} %copy-done) | copy-start | bytes 3145732
  406.2 12.8 %copy-start.51 = (pred[256,256]{0,1:T(8,128)(4,1)S(1)}, pred[256,256]{0,1:T(8,128)(4,1)}, u32[]{:S(2)}) copy-start(pred[256,256]{0,1:T(8,128)(4,1)} %copy-done.50) | copy-start | bytes 196612
  413.5 74.7 %collective-permute-start.18 = (bf16[256,1024]{1,0:T(8,128)(2,1)}, bf16[256,1024]{1,0:T(8,128)(2,1)}, u32[]{:S(2)}, u32[]{:S(2)}) collective-permute-start(bf16[256,1024]{1,0:T(8,128)(2,1)} %pad_maximum_fusion.4), channel_id=1, source_target_pairs={{20,0},{24,4},{28,8},{32,12},{36,16},{40,20},{44,24},{48,28},{52,3... | collective-permute-start | bytes 1572872 | tf_op jit(solution)/shard_map/ppermute | solution.py:20
  442.1 78.5 %reduce-scatter.8.cloned.1.call-start = ((), (), s32[]{:S(2)}) async-start(), calls=%async_computation.6 | async-start | bytes 393216 | tf_op jit(solution)/shard_map/reduce_scatter | solution.py:112
  448.4 14.7 %copy-start.27 = (bf16[256,512]{0,1:T(8,128)(2,1)S(1)}, bf16[256,512]{0,1:T(8,128)(2,1)}, u32[]{:S(2)}) copy-start(bf16[256,512]{0,1:T(8,128)(2,1)} %copy-done.26) | copy-start | bytes 786436
  448.4 14.7 %copy-start.44 = (f32[256,4,128]{0,2,1:T(8,128)S(1)}, f32[256,4,128]{0,2,1:T(8,128)}, u32[]{:S(2)}) copy-start(f32[256,4,128]{0,2,1:T(8,128)} %fusion.61) | copy-start | bytes 1572868
  448.4 14.7 %copy-start.45 = (f32[256,4,128]{0,2,1:T(8,128)S(1)}, f32[256,4,128]{0,2,1:T(8,128)}, u32[]{:S(2)}) copy-start(f32[256,4,128]{0,2,1:T(8,128)} %fusion.60) | copy-start | bytes 1572868
  448.4 14.7 %copy-start.46 = (f32[256,4,128]{0,2,1:T(8,128)S(1)}, f32[256,4,128]{0,2,1:T(8,128)}, u32[]{:S(2)}) copy-start(f32[256,4,128]{0,2,1:T(8,128)} %fusion.59) | copy-start | bytes 1572868
  449.5 39.9 %collective-permute-start.19 = (bf16[256,1024]{1,0:T(8,128)(2,1)}, bf16[256,1024]{1,0:T(8,128)(2,1)S(1)}, u32[]{:S(2)}, u32[]{:S(2)}) collective-permute-start(bf16[256,1024]{1,0:T(8,128)(2,1)} %pad_maximum_fusion.5), channel_id=1, source_target_pairs={{24,0},{28,4},{32,8},{36,12},{40,16},{44,20},{48,24},{52,28},{56,3... | collective-permute-start | bytes 1572872 | tf_op jit(solution)/shard_map/ppermute | solution.py:20
  457.6 37.9 %collective-permute-start.20 = (bf16[256,1024]{1,0:T(8,128)(2,1)}, bf16[256,1024]{1,0:T(8,128)(2,1)}, u32[]{:S(2)}, u32[]{:S(2)}) collective-permute-start(bf16[256,1024]{1,0:T(8,128)(2,1)} %pad_maximum_fusion.6), channel_id=1, source_target_pairs={{28,0},{32,4},{36,8},{40,12},{44,16},{48,20},{52,24},{56,28},{60,3... | collective-permute-start | bytes 1572872 | tf_op jit(solution)/shard_map/ppermute | solution.py:20
  461.1 56.5 %collective-permute-start.21 = (bf16[256,1024]{1,0:T(8,128)(2,1)}, bf16[256,1024]{1,0:T(8,128)(2,1)}, u32[]{:S(2)}, u32[]{:S(2)}) collective-permute-start(bf16[256,1024]{1,0:T(8,128)(2,1)} %pad_maximum_fusion.7), channel_id=1, source_target_pairs={{32,0},{36,4},{40,8},{44,12},{48,16},{52,20},{56,24},{60,28},{64,3... | collective-permute-start | bytes 1572872 | tf_op jit(solution)/shard_map/ppermute | solution.py:20
  489.4 29.4 %copy-start.43 = (f32[256,512]{1,0:T(8,128)S(1)}, f32[256,512]{1,0:T(8,128)}, u32[]{:S(2)}) copy-start(f32[256,512]{1,0:T(8,128)} %copy.490) | copy-start | bytes 1572868
  (75 other events, 262.1 us)
Sparse Core Ops, SparseCore 0:
  35.5 24.5 all-gather.1
  217.5 117.5 reduce-scatter.3
  442.2 39.9 reduce-scatter.5
  485.1 17.1 reduce-scatter.7
